TPU v7x, 32 devices: a whole 2x2x4 slice. The times are simulated.
32 devices in a mesh: phase: 4 (over y, x), rows: 8 (over z, core).
Axes of the slice: x: 2, y: 2, z: 4, core: 2. Of those that a mesh axis runs over, the one named last changes fastest.
Arguments:
- frames: bfloat16 [2, 192, 16, 128], P(None, None, 'rows'), may hold values from -12 to 12, as said below
- causal_cache: bfloat16 [4, 2, 2, 192, 16, 128], P('phase', None, None, None, 'rows'), may hold values from -4 to 4
- conv_weight: bfloat16 [4, 2, 3, 3, 3, 192, 192], P('phase'), may hold values from -0.15625 to 0.15625
- conv_bias: float32 [4, 2, 192], P('phase'), may hold values from -3 to 3
- norm_gain: float32 [4, 2, 192], P('phase'), may hold values from 0.1 to 1.9
- norm_shift: float32 [4, 2, 192], P('phase'), may hold values from -3 to 3
Outputs:
- phase_out: bfloat16 [4, 2, 192, 16, 128], P('phase', None, None, 'rows')
- new_cache: bfloat16 [4, 2, 2, 192, 16, 128], P('phase', None, None, None, 'rows')
Inputs may be any that keep to these rules, and one draw needn't show every extreme that they name: `frames`: Real-valued frame features.
All inputs are finite; a program needn't handle non-finite values.
Results may differ from a plain program's by a relative error of at most 0.0066.
Values may be sent and summed in bfloat16 or wider, within the bound.
No kernel may reach another device: no remote copies, remote signals or barrier semaphores. Data moves between devices by JAX's collectives and lax.ppermute only.
A program may use at most 64 MiB of HBM per device.

v0:
```python
import jax
import jax.numpy as jnp
from jax import lax
from jax.sharding import PartitionSpec as P
from jax.experimental import pallas as pl
from jax.experimental.pallas import tpu as pltpu
import functools

GROUPS = 32
EPS = 1e-06
MAX_SPAN = 16


def span_devices(peers, rows_here):
    count = 1
    while count * 2 <= peers and peers % (count * 2) == 0 and count * 2 * rows_here <= MAX_SPAN:
        count *= 2
    return count


def gather_span(array, dim, span_count):
    if span_count == 1:
        return array
    peers = lax.axis_size("rows")
    if span_count == peers:
        return lax.all_gather(array, "rows", axis=dim, tiled=True)
    place = lax.axis_index("rows") % span_count
    pieces = [array]
    for shift in range(1, span_count):
        pairs = [
            (b * span_count + p, b * span_count + (p + shift) % span_count)
            for b in range(peers // span_count)
            for p in range(span_count)
        ]
        pieces.append(lax.ppermute(array, "rows", pairs))
    stacked = jnp.stack(pieces)
    order = (place - jnp.arange(span_count)) % span_count
    picked = jnp.take(stacked, order, axis=0)
    picked = jnp.moveaxis(picked, 0, dim)
    shape = list(array.shape)
    shape[dim] = shape[dim] * span_count
    return picked.reshape(shape)


def with_rim(array, dim, span_count):
    peers = lax.axis_size("rows")
    length = array.shape[dim]
    if span_count == peers:
        return array
    up = [(i, i + span_count) for i in range(peers - span_count)]
    down = [(j, i) for i, j in up]
    last = lax.slice_in_dim(array, length - 1, length, axis=dim)
    leading = lax.slice_in_dim(array, 0, 1, axis=dim)
    before = lax.ppermute(last, "rows", up)
    after = lax.ppermute(leading, "rows", down)
    return jnp.concatenate([before, array, after], axis=dim)


def pass_on(result, span_count):
    phase_count = lax.axis_size("phase")
    forward = [(s, s + 1) for s in range(phase_count - 1)]
    length = result.shape[0]
    if span_count % 2 or length % 2:
        return lax.ppermute(result, "phase", forward)
    peers = lax.axis_size("rows")
    half = length // 2
    core = lax.axis_index("rows") % 2
    mine = lax.dynamic_slice_in_dim(result, core * half, half, axis=0)
    got = lax.ppermute(mine, "phase", forward)
    other = lax.ppermute(got, "rows", [(i, i ^ 1) for i in range(peers)])
    return jnp.where(core == 0, jnp.concatenate([got, other]), jnp.concatenate([other, got]))


def arrange_taps(weight):
    outputs = weight.shape[3]
    channels = weight.shape[4]
    return jnp.transpose(weight, (2, 3, 0, 1, 4)).reshape(3 * outputs, 9 * channels)


def conv_rows(x0, x1, x2, taps, bias, res, out, rows_out, padded):
    outputs = out.shape[1]
    channels = x0.shape[1]
    columns = x0.shape[2]
    pair = 4 if rows_out % 4 == 0 else (2 if rows_out % 2 == 0 else 1)
    lanes = pair * columns
    lane = lax.broadcasted_iota(jnp.int32, (outputs, lanes), 1) % columns
    frames = (x0, x1, x2)

    def column(r):
        if padded or 0 < r < rows_out - 1:
            base = r if padded else r - 1
            parts = [x[pl.ds(base, 3)] for x in frames]
            return jnp.concatenate(parts, axis=0).reshape(9 * channels, columns)
        zero = jnp.zeros((1, channels, columns), x0.dtype)
        parts = []
        for x in frames:
            for dy in range(3):
                q = r + dy - 1
                parts.append(zero if q < 0 or q >= rows_out else x[pl.ds(q, 1)])
        return jnp.concatenate(parts, axis=0).reshape(9 * channels, columns)

    for r in range(0, rows_out, pair):
        cols = [column(r + k) for k in range(pair)]
        rhs = cols[0] if pair == 1 else jnp.concatenate(cols, axis=1)
        acc = jnp.dot(taps[...], rhs, preferred_element_type=jnp.float32)
        left = pltpu.roll(acc[:outputs], 1, 1)
        right = pltpu.roll(acc[2 * outputs :], lanes - 1, 1)
        total = acc[outputs : 2 * outputs] + jnp.where(lane == 0, 0.0, left)
        total = total + jnp.where(lane == columns - 1, 0.0, right) + bias[...]
        for k in range(pair):
            piece = total[:, k * columns : (k + 1) * columns]
            if res is not None:
                piece = piece + res[r + k].astype(jnp.float32)
            out[r + k] = piece.astype(out.dtype)


def conv_body(x0, x1, x2, taps, bias, *rest, rows_out, with_res, padded):
    res = rest[0] if with_res else None
    conv_rows(x0, x1, x2, taps, bias, res, rest[-1], rows_out, padded)


def causal_conv(x0, x1, x2, taps, bias_vec, res, padded):
    rows_out = x0.shape[0] - 2 if padded else x0.shape[0]
    outputs = taps.shape[0] // 3
    args = [x0, x1, x2, taps, bias_vec.reshape(outputs, 1)]
    if res is not None:
        args.append(res)
    body = functools.partial(conv_body, rows_out=rows_out, with_res=res is not None, padded=padded)
    shape = jax.ShapeDtypeStruct((rows_out, outputs, x0.shape[2]), jnp.bfloat16)
    return pl.pallas_call(body, out_shape=shape)(*args)


def conv_span(x0, x1, x2, taps, bias, res, out, base, count):
    outputs = out.shape[1]
    channels = x0.shape[1]
    columns = x0.shape[2]
    pair = next(p for p in (16, 8, 4, 2, 1) if count % p == 0)
    lanes = pair * columns
    lane = lax.broadcasted_iota(jnp.int32, (outputs, lanes), 1) % columns

    def step(i, carry):
        r = base + i * pair
        cols = []
        for k in range(pair):
            parts = [x[pl.ds(r + k, 3)] for x in (x0, x1, x2)]
            cols.append(jnp.concatenate(parts, axis=0).reshape(9 * channels, columns))
        rhs = cols[0] if pair == 1 else jnp.concatenate(cols, axis=1)
        acc = jnp.dot(taps[...], rhs, preferred_element_type=jnp.float32)
        left = pltpu.roll(acc[:outputs], 1, 1)
        right = pltpu.roll(acc[2 * outputs :], lanes - 1, 1)
        total = acc[outputs : 2 * outputs] + jnp.where(lane == 0, 0.0, left)
        total = total + jnp.where(lane == columns - 1, 0.0, right) + bias[...]
        for k in range(pair):
            piece = total[:, k * columns : (k + 1) * columns]
            if res is not None:
                piece = piece + res[r + k].astype(jnp.float32)
            out[i * pair + k] = piece.astype(out.dtype)
        return carry

    lax.fori_loop(0, count // pair, step, 0)


def fused_body(flags, caches, a_p, a_pp, frames, src_b, src_c, taps, bias, member, gain, shift, *rest,
               kind, tick, frame_at, cache_at):
    rest = list(rest)
    own = rest.pop(0) if kind != "first" else None
    if kind == "tail":
        out, x0, x1, rawbuf, tapbuf, sems = rest
        act = own
    else:
        out, act, x0, x1, rawbuf, tapbuf, sems = rest
    span, channels, columns = rawbuf.shape
    half = span // 2
    first, second, mode, core = flags[tick, 0], flags[tick, 1], flags[tick, 2], flags[tick, 3]
    c0, c1 = caches.at[cache_at[0]], caches.at[cache_at[1]]
    whole = frames.at[frame_at]
    top, bottom = rawbuf.at[pl.ds(0, half)], rawbuf.at[pl.ds(half, half)]
    inner0, inner1 = x0.at[pl.ds(1, span)], x1.at[pl.ds(1, span)]

    def inner(x):
        return x.at[pl.ds(1, span)]

    def begin(pairs, base):
        for i, (a, b) in enumerate(pairs):
            pltpu.make_async_copy(a, b, sems.at[base + i]).start()

    def finish(pairs, base):
        for i, (a, b) in enumerate(pairs):
            pltpu.make_async_copy(a, b, sems.at[base + i]).wait()

    pltpu.make_async_copy(taps, tapbuf, sems.at[4]).start()

    @pl.when(mode == 0)
    def _():
        begin([(whole.at[pl.ds(0, half)], top), (whole.at[pl.ds(half, half)], bottom)], 0)

    @pl.when(mode == 1)
    def _():
        begin([(src_b, top), (src_c, bottom)], 0)

    @pl.when(mode == 2)
    def _():
        begin([(src_c, top), (src_b, bottom)], 0)

    @pl.when(first == 1)
    def _():
        begin([(c0, inner0), (c1, inner1)], 2)

    @pl.when(jnp.logical_and(first == 0, second == 1))
    def _():
        begin([(c1, inner0), (inner(a_p), inner1)], 2)

    @pl.when(jnp.logical_and(first == 0, second == 0))
    def _():
        begin([(inner(a_pp), inner0), (inner(a_p), inner1)], 2)

    zero = jnp.zeros((channels, columns), x0.dtype)
    for x in (x0, x1):
        x[0] = zero
        x[span + 1] = zero
    source_copies = [(src_b, top), (src_c, bottom)]
    history_copies = [(inner(a_pp), inner0), (inner(a_p), inner1)]

    if kind != "tail":
        if kind == "first":
            finish(source_copies, 0)
            raw = rawbuf
        else:
            raw = own
        count = float(span * columns * (channels // GROUPS))

        def group_total(acc):
            spread = jnp.dot(member[...], acc, precision=lax.Precision.HIGHEST, preferred_element_type=jnp.float32)
            return jnp.sum(spread, axis=1, keepdims=True)

        acc = raw[0].astype(jnp.float32)
        for r in range(1, span):
            acc = acc + raw[r].astype(jnp.float32)
        average = group_total(acc) / count
        acc = jnp.square(raw[0].astype(jnp.float32) - average)
        for r in range(1, span):
            acc = acc + jnp.square(raw[r].astype(jnp.float32) - average)
        inverse = lax.rsqrt(group_total(acc) / count + EPS)
        act[0] = zero
        act[span + 1] = zero
        for r in range(span):
            value = (raw[r].astype(jnp.float32) - average) * inverse
            value = value * gain[...] + shift[...]
            act[r + 1] = (value / (1.0 + jnp.exp(-value))).astype(act.dtype)

    finish(history_copies, 2)
    pltpu.make_async_copy(taps, tapbuf, sems.at[4]).wait()
    taps = tapbuf
    if kind == "first":
        conv_span(x0, x1, act, taps, bias, None, out, 0, span)
    elif kind == "all":
        finish(source_copies, 0)
        conv_span(x0, x1, act, taps, bias, rawbuf, out, 0, span)
    else:
        finish(source_copies, 0)
        base = core * half if kind == "lead" else (1 - core) * half
        conv_span(x0, x1, act, taps, bias, rawbuf, out, base, half)


def fused_conv(flags, tick, caches, cache_at, recent, frames, frame_at, halves, taps, bias_vec, norm, kind, own=None):
    span, channels, columns = caches.shape[1:]
    outputs = taps.shape[0] // 3
    group_of = jnp.arange(channels) // (channels // GROUPS)
    member = (group_of[:, None] == group_of[None, :]).astype(jnp.float32)
    vmem = pl.BlockSpec(memory_space=pltpu.VMEM)
    anywhere = pl.BlockSpec(memory_space=pl.ANY)
    args = [flags, caches, recent[0], recent[1], frames, halves[0], halves[1]]
    args += [taps, bias_vec.reshape(outputs, 1), member]
    args += [v.reshape(-1, 1).astype(jnp.float32) for v in norm]
    specs = [pl.BlockSpec(memory_space=pltpu.SMEM)] + [anywhere] * 7 + [vmem] * 4
    if own is not None:
        args.append(own)
        specs.append(vmem)
    rows_out = span if kind in ("first", "all") else span // 2
    result = jax.ShapeDtypeStruct((rows_out, outputs, columns), jnp.bfloat16)
    padded = jax.ShapeDtypeStruct((span + 2, channels, columns), jnp.bfloat16)
    shapes = result if kind == "tail" else (result, padded)
    body = functools.partial(
        fused_body, kind=kind, tick=tick, frame_at=frame_at, cache_at=tuple(cache_at)
    )
    return pl.pallas_call(
        body,
        out_shape=shapes,
        in_specs=specs,
        out_specs=vmem if kind == "tail" else (vmem, vmem),
        scratch_shapes=[
            pltpu.VMEM((span + 2, channels, columns), jnp.bfloat16),
            pltpu.VMEM((span + 2, channels, columns), jnp.bfloat16),
            pltpu.VMEM((span, channels, columns), jnp.bfloat16),
            pltpu.VMEM(taps.shape, taps.dtype),
            pltpu.SemaphoreType.DMA((5,)),
        ],
    )(*args)


def block_sum(values, span_count):
    peers = lax.axis_size("rows")
    if span_count == peers:
        return values
    lead = (lax.axis_index("rows") % span_count == 0).astype(values.dtype)
    return lax.psum(values * lead, "rows")


def activate(source, gain_vec, shift_vec, cell_count, span_count):
    height, channels, columns = source.shape
    grouped = source.astype(jnp.float32).reshape(height, GROUPS, channels // GROUPS, columns)
    average = block_sum(jnp.sum(grouped, axis=(0, 2, 3)), span_count) / cell_count
    centred = grouped - average[None, :, None, None]
    spread = block_sum(jnp.sum(centred * centred, axis=(0, 2, 3)), span_count) / cell_count
    inverse = lax.rsqrt(spread + EPS)
    normed = (centred * inverse[None, :, None, None]).reshape(height, channels, columns)
    normed = normed * gain_vec[None, :, None] + shift_vec[None, :, None]
    return jax.nn.silu(normed).astype(jnp.bfloat16)


def run_frame(source, first_hist, second_hist, kernels, biases, gains, shifts, cell_count, span_count):
    padded = span_count != lax.axis_size("rows")
    first_in = with_rim(activate(source, gains[0], shifts[0], cell_count, span_count), 0, span_count)
    hidden = causal_conv(first_hist[0], first_hist[1], first_in, kernels[0], biases[0], None, padded)
    second_in = with_rim(activate(hidden, gains[1], shifts[1], cell_count, span_count), 0, span_count)
    result = causal_conv(second_hist[0], second_hist[1], second_in, kernels[1], biases[1], source, padded)
    return (result, (first_hist[1], first_in), (second_hist[1], second_in))


def shards_whole(frames, causal_cache, conv_weight, conv_bias, norm_gain, norm_shift):
    phase_no = lax.axis_index("phase")
    phase_count = lax.axis_size("phase")
    peers = lax.axis_size("rows")
    frame_count, channels, rows_here, columns = frames.shape
    span = rows_here * peers
    half = span // 2
    core = lax.axis_index("rows") % 2
    start = lax.axis_index("rows") * rows_here
    forward = [(s, s + 1) for s in range(phase_count - 1)]
    frames_t = jnp.transpose(frames, (0, 2, 1, 3))
    cache_t = jnp.transpose(causal_cache[0], (0, 1, 3, 2, 4))
    early = lax.all_gather(jnp.stack([frames_t[0], cache_t[0, 0], cache_t[0, 1]]), "rows", axis=1, tiled=True)
    second_cache = lax.all_gather(cache_t[1], "rows", axis=1, tiled=True)
    later = list(frames_t[1:])
    if len(later) == 1:
        later = later * 2
    later = lax.all_gather(jnp.stack(later), "rows", axis=1, tiled=True) if later else early
    frame_of = [(early, 0)] + [(later, f) for f in range(frame_count - 1)]
    cache_of = ((early, (1, 2)), (second_cache, (0, 1)))
    taps = (arrange_taps(conv_weight[0, 0]), arrange_taps(conv_weight[0, 1]))

    def own_rows(x, rim=0):
        return lax.dynamic_slice_in_dim(x, start + rim, rows_here, axis=0)

    got = other = jnp.zeros((half, channels, columns), jnp.bfloat16)
    acts = ([], [])
    blank = jnp.zeros((rows_here, channels, columns), jnp.bfloat16)
    blank_frame = jnp.zeros((span + 2, channels, columns), jnp.bfloat16)
    produced = [blank] * frame_count
    kept = [[blank, blank], [blank, blank]]
    mode = jnp.where(phase_no == 0, 0, 1 + core)
    tick_count = frame_count + phase_count - 1
    frame_nos = jnp.arange(tick_count) - phase_no
    flags = jnp.stack(
        [frame_nos == 0, frame_nos == 1, jnp.full((tick_count,), mode), jnp.full((tick_count,), core)], axis=1
    ).astype(jnp.int32)
    for tick_no in range(tick_count):
        frame_no = tick_no - phase_no
        frame_stack, frame_at = frame_of[min(tick_no, frame_count - 1)]
        recents = []
        for j in range(2):
            a_p = acts[j][-1] if acts[j] else blank_frame
            a_pp = acts[j][-2] if len(acts[j]) > 1 else blank_frame
            recents.append((a_p, a_pp))
        common = (frame_stack, frame_at, (got, other))
        hidden, first_in = fused_conv(
            flags, tick_no, cache_of[0][0], cache_of[0][1], recents[0], *common,
            taps[0], conv_bias[0, 0], (norm_gain[0, 0], norm_shift[0, 0]), "first",
        )
        second = (flags, tick_no, cache_of[1][0], cache_of[1][1], recents[1], *common, taps[1], conv_bias[0, 1])
        if tick_no + 1 == tick_count:
            whole_out, second_in = fused_conv(*second, (norm_gain[0, 1], norm_shift[0, 1]), "all", hidden)
            lead = lax.dynamic_slice_in_dim(whole_out, core * half, half, axis=0)
            tail = lax.dynamic_slice_in_dim(whole_out, (1 - core) * half, half, axis=0)
        else:
            lead, second_in = fused_conv(*second, (norm_gain[0, 1], norm_shift[0, 1]), "lead", hidden)
            tail = fused_conv(*second, (norm_gain[0, 1], norm_shift[0, 1]), "tail", second_in)
        if tick_no + 1 < tick_count:
            got = lax.ppermute(lead, "phase", forward)
            got, tail = lax.optimization_barrier((got, tail))
            other = lax.ppermute(got, "rows", [(i, i ^ 1) for i in range(peers)])
        last = frame_no == frame_count - 1
        for j, a in enumerate((first_in, second_in)):
            stack, (_, k1) = cache_of[j]
            newer = jnp.where(frame_no == 0, own_rows(stack[k1]), own_rows(recents[j][0], 1))
            kept[j] = [jnp.where(last, newer, kept[j][0]), jnp.where(last, own_rows(a, 1), kept[j][1])]
            acts[j].append(a)
        mine = lax.dynamic_slice_in_dim(lead, start - core * half, rows_here, axis=0)
        theirs = lax.dynamic_slice_in_dim(tail, start - (1 - core) * half, rows_here, axis=0)
        result_rows = jnp.where(start // half == core, mine, theirs)
        for f in range(frame_count):
            if 0 <= tick_no - f < phase_count:
                produced[f] = jnp.where(frame_no == f, result_rows, produced[f])
    produced = jnp.transpose(jnp.stack(produced), (0, 2, 1, 3))
    new_cache = jnp.transpose(jnp.stack([jnp.stack(k) for k in kept]), (0, 1, 3, 2, 4))
    return (produced[None], new_cache[None])


def shards(frames, causal_cache, conv_weight, conv_bias, norm_gain, norm_shift):
    peers = lax.axis_size("rows")
    rows_here = frames.shape[2]
    if span_devices(peers, rows_here) == peers and (rows_here * peers) % 2 == 0:
        return shards_whole(frames, causal_cache, conv_weight, conv_bias, norm_gain, norm_shift)
    return shards_split(frames, causal_cache, conv_weight, conv_bias, norm_gain, norm_shift)


def shards_split(frames, causal_cache, conv_weight, conv_bias, norm_gain, norm_shift):
    phase_no = lax.axis_index("phase")
    phase_count = lax.axis_size("phase")
    peers = lax.axis_size("rows")
    frame_count = frames.shape[0]
    channels = frames.shape[1]
    rows_here = frames.shape[2]
    columns = frames.shape[3]
    span_count = span_devices(peers, rows_here)
    span = rows_here * span_count
    cell_count = float(channels // GROUPS * rows_here * peers * columns)
    padded = span_count != peers
    frames_t = jnp.transpose(frames, (0, 2, 1, 3))
    cache_t = jnp.transpose(causal_cache[0], (0, 1, 3, 2, 4))
    early = gather_span(jnp.stack([frames_t[0], cache_t[0, 0], cache_t[0, 1]]), 1, span_count)
    late = gather_span(jnp.stack([cache_t[1, 0], cache_t[1, 1]] + list(frames_t[1:])), 1, span_count)
    frames_span = [early[0]] + [late[2 + f] for f in range(frame_count - 1)]
    first_hist = tuple(with_rim(early[1 + k], 0, span_count) for k in range(2))
    second_hist = tuple(with_rim(late[k], 0, span_count) for k in range(2))
    local_taps = (arrange_taps(conv_weight[0, 0]), arrange_taps(conv_weight[0, 1]))
    incoming = jnp.zeros_like(frames_span[0])
    produced = [jnp.zeros_like(frames_span[0]) for _ in range(frame_count)]
    tick_count = frame_count + phase_count - 1
    for tick_no in range(tick_count):
        frame_no = tick_no - phase_no
        active_now = jnp.logical_and(frame_no >= 0, frame_no < frame_count)
        source = jnp.where(phase_no == 0, frames_span[min(tick_no, frame_count - 1)], incoming)
        result, first_next, second_next = run_frame(
            source, first_hist, second_hist, local_taps, conv_bias[0], norm_gain[0], norm_shift[0],
            cell_count, span_count,
        )
        first_hist = tuple(jnp.where(active_now, a, b) for a, b in zip(first_next, first_hist))
        second_hist = tuple(jnp.where(active_now, a, b) for a, b in zip(second_next, second_hist))
        for f in range(frame_count):
            if 0 <= tick_no - f < phase_count:
                produced[f] = jnp.where(frame_no == f, result, produced[f])
        if tick_no + 1 < tick_count:
            incoming = pass_on(result, span_count)
    start = (lax.axis_index("rows") % span_count) * rows_here
    rim = 1 if padded else 0
    produced = jnp.stack([lax.dynamic_slice_in_dim(p, start, rows_here, axis=0) for p in produced])
    new_cache = jnp.stack(
        [
            jnp.stack([lax.dynamic_slice_in_dim(h, start + rim, rows_here, axis=0) for h in hist])
            for hist in (first_hist, second_hist)
        ]
    )
    produced = jnp.transpose(produced, (0, 2, 1, 3))
    new_cache = jnp.transpose(new_cache, (0, 1, 3, 2, 4))
    return (produced[None], new_cache[None])


def solution(mesh):
    in_specs = (
        P(None, None, "rows", None),
        P("phase", None, None, None, "rows", None),
        P("phase", None, None, None, None, None, None),
        P("phase", None, None),
        P("phase", None, None),
        P("phase", None, None),
    )
    out_specs = (P("phase", None, None, "rows", None), P("phase", None, None, None, "rows", None))
    return jax.shard_map(shards, mesh=mesh, in_specs=in_specs, out_specs=out_specs, check_vma=False)
```

profile of v0, /device:TPU:4, one launch (start us, length us, event | category | flops | bytes accessed | tf_op | source)
XLA Modules:
  0.0 230.4 jit_solution(6368089026698132218)
XLA Ops:
  7.2 1.0 copy.64
  8.3 1.0 copy.65
  12.8 4.7 %slice_bitcast_fusion = (bf16[3,192,3,3,192]{4,1,0,3,2:T(8,128)(2,1)S(1)}, bf16[3,192,3,3,192]{4,1,0,3,2:T(8,128)(2,1)}) fusion(bf16[1,2,3,3,3,192,192]{6,5,4,3,2,1,0:T(8,128)(2,1)} %param.8), kind=kLoop, calls=%fused_computation | loop fusion | bytes 7962624 | tf_op jit(solution)/shard_map/transpose | solution.py:77
  17.5 2.3 copy.17
  19.8 4.4 %reshape.59.taps = bf16[576,1728]{1,0:T(8,128)(2,1)} reshape(bf16[3,192,3,3,192]{4,3,2,1,0:T(4,128)(2,1)S(1)} %copy.17) | data formatting | bytes 3981312 | tf_op jit(solution)/shard_map/reshape | solution.py:77
  24.2 0.8 copy.18.bias
  25.0 0.8 copy.19.gain
  26.5 4.1 %copy.16 = bf16[3,192,3,3,192]{4,3,2,1,0:T(4,128)(2,1)S(1)} copy(bf16[3,192,3,3,192]{4,1,0,3,2:T(8,128)(2,1)} %get-tuple-element.63) | data formatting | bytes 3981312 | tf_op jit(solution)/shard_map/transpose | solution.py:77
  30.6 4.2 %reshape.58.taps = bf16[576,1728]{1,0:T(8,128)(2,1)} reshape(bf16[3,192,3,3,192]{4,3,2,1,0:T(4,128)(2,1)S(1)} %copy.16) | data formatting | bytes 3981312 | tf_op jit(solution)/shard_map/reshape | solution.py:77
  34.9 0.8 copy.21.bias
  37.2 1.3 add_add_fusion.flags
  38.5 0.8 compare_convert_fusion.member
  39.3 3.8 %all-gather.5.cloned.1.call-done.caches.frames = bf16[3,16,192,128]{3,2,1,0:T(8,128)(2,1)} async-done(((bf16[3,2,192,128]{3,2,1,0:T(8,128)(2,1)}), bf16[3,16,192,128]{3,2,1,0:T(8,128)(2,1)}) %all-gather.5.cloned.1.call-update) | async-done | bytes 2359312 | tf_op jit(solution)/shard_map/all_gather | solution.py:342
  43.0 1.2 broadcast_in_dim.8.a_p.a_pp
  44.2 0.8 broadcast_in_dim.9.src_b.src_c
  45.0 10.7 %shard_map.77 = (bf16[16,192,128]{2,1,0:T(8,128)(2,1)}, bf16[18,192,128]{2,1,0:T(8,128)(2,1)}) custom-call(s32[5,4]{1,0:T(8,128)} %add_add_fusion.flags, bf16[3,16,192,128]{3,2,1,0:T(8,128)(2,1)} %all-gather.5.cloned.1.call-done.caches.frames, bf16[18,192,128]{2,1,0:T(8,128)(2,1)} %broadcast_in_dim.8.a_p.a_pp, ...), custom_call_target="tpu_custom_call" | custom-call | tf_op jit(solution)/shard_map/pallas_call | solution.py:286
  55.7 13.8 %all-gather.9.cloned.1.call-done = bf16[1,2,16,192,128]{4,3,2,1,0:T(8,128)(2,1)} async-done(((bf16[1,2,2,192,128]{4,3,2,1,0:T(8,128)(2,1)}), bf16[1,2,16,192,128]{4,3,2,1,0:T(8,128)(2,1)}) %all-gather.9.cloned.1.call-update) | async-done | bytes 1572880 | tf_op jit(solution)/shard_map/all_gather | solution.py:343
  69.4 6.9 %shard_map.78 = (bf16[8,192,128]{2,1,0:T(8,128)(2,1)}, bf16[18,192,128]{2,1,0:T(8,128)(2,1)}) custom-call(s32[5,4]{1,0:T(8,128)} %add_add_fusion.flags, bf16[2,16,192,128]{3,2,1,0:T(8,128)(2,1)} %bitcast.111, bf16[18,192,128]{2,1,0:T(8,128)(2,1)} %broadcast_in_dim.8.a_p.a_pp, bf16[18,192,128]{2,1,0:T(8,128)(2,1)} %broadcast_in_dim.8.a_p.a_pp, ...), custom_call_target="tpu_custom_call" | custom-call | tf_op jit(solution)/shard_map/pallas_call | solution.py:286
  76.3 3.6 %collective-permute-start = (bf16[8,192,128]{2,1,0:T(8,128)(2,1)}, bf16[8,192,128]{2,1,0:T(8,128)(2,1)S(1)}, u32[]{:S(2)}, u32[]{:S(2)}) collective-permute-start(bf16[8,192,128]{2,1,0:T(8,128)(2,1)} %get-tuple-element.32), channel_id=1, source_target_pairs={{0,8},{8,16},{16,24},{1,9},{9,17},{17,25},{2,10},{10,18},{18,26},{... | collective-permute-start | bytes 1179656 | tf_op jit(solution)/shard_map/ppermute | solution.py:389
  79.9 6.9 %shard_map.79 = bf16[8,192,128]{2,1,0:T(8,128)(2,1)} custom-call(s32[5,4]{1,0:T(8,128)} %add_add_fusion.flags, bf16[2,16,192,128]{3,2,1,0:T(8,128)(2,1)} %bitcast.112, bf16[18,192,128]{2,1,0:T(8,128)(2,1)} %broadcast_in_dim.8.a_p.a_pp, bf16[18,192,128]{2,1,0:T(8,128)(2,1)} %broadcast_in_dim.8.a_p.a_pp, ...), custom_call_target="tpu_custom_call" | custom-call | tf_op jit(solution)/shard_map/pallas_call | solution.py:286
  86.8 3.7 %collective-permute-done.src_b = bf16[8,192,128]{2,1,0:T(8,128)(2,1)S(1)} collective-permute-done((bf16[8,192,128]{2,1,0:T(8,128)(2,1)}, bf16[8,192,128]{2,1,0:T(8,128)(2,1)S(1)}, u32[]{:S(2)}, u32[]{:S(2)}) %collective-permute-start) | collective-permute-done | bytes 393248 | tf_op jit(solution)/shard_map/ppermute | solution.py:389
  90.6 5.1 %all-gather.7.cloned.1.call-done.frames = bf16[2,16,192,128]{3,2,1,0:T(8,128)(2,1)} async-done(((bf16[2,2,192,128]{3,2,1,0:T(8,128)(2,1)}), bf16[2,16,192,128]{3,2,1,0:T(8,128)(2,1)}) %all-gather.7.cloned.1.call-update) | async-done | bytes 1572880 | tf_op jit(solution)/shard_map/all_gather | solution.py:347
  96.4 10.2 %shard_map.80 = (bf16[16,192,128]{2,1,0:T(8,128)(2,1)}, bf16[18,192,128]{2,1,0:T(8,128)(2,1)}) custom-call(s32[5,4]{1,0:T(8,128)} %add_add_fusion.flags, bf16[3,16,192,128]{3,2,1,0:T(8,128)(2,1)} %all-gather.5.cloned.1.call-done.caches.frames, bf16[18,192,128]{2,1,0:T(8,128)(2,1)} %get-tuple-element.34.a_p.a_pp, ...), custom_call_target="tpu_custom_call" | custom-call | tf_op jit(solution)/shard_map/pallas_call | solution.py:286
  106.7 6.9 %shard_map.81 = (bf16[8,192,128]{2,1,0:T(8,128)(2,1)}, bf16[18,192,128]{2,1,0:T(8,128)(2,1)}) custom-call(s32[5,4]{1,0:T(8,128)} %add_add_fusion.flags, bf16[2,16,192,128]{3,2,1,0:T(8,128)(2,1)} %bitcast.113, bf16[18,192,128]{2,1,0:T(8,128)(2,1)} %get-tuple-element.31.rest_0_.a_p.a_pp, bf16[18,192,128]{2,1,0:T(8,128)(2,1)} %broadcast_in_dim.8.a_p.a_pp, ...), custom_call_target="tpu_custom_call" | custom-call | tf_op jit(solution)/shard_map/pallas_call | solution.py:286
  113.6 3.8 %collective-permute-start.2 = (bf16[8,192,128]{2,1,0:T(8,128)(2,1)}, bf16[8,192,128]{2,1,0:T(8,128)(2,1)S(1)}, u32[]{:S(2)}, u32[]{:S(2)}) collective-permute-start(bf16[8,192,128]{2,1,0:T(8,128)(2,1)} %get-tuple-element.37), channel_id=1, source_target_pairs={{0,8},{8,16},{16,24},{1,9},{9,17},{17,25},{2,10},{10,18},{18,26},{... | collective-permute-start | bytes 1179656 | tf_op jit(solution)/shard_map/ppermute | solution.py:389
  117.4 6.9 %shard_map.82 = bf16[8,192,128]{2,1,0:T(8,128)(2,1)} custom-call(s32[5,4]{1,0:T(8,128)} %add_add_fusion.flags, bf16[2,16,192,128]{3,2,1,0:T(8,128)(2,1)} %bitcast.114, bf16[18,192,128]{2,1,0:T(8,128)(2,1)} %get-tuple-element.31.rest_0_.a_p.a_pp, bf16[18,192,128]{2,1,0:T(8,128)(2,1)} %broadcast_in_dim.8.a_p.a_pp, ...), custom_call_target="tpu_custom_call" | custom-call | tf_op jit(solution)/shard_map/pallas_call | solution.py:286
  124.3 3.5 %collective-permute-done.2.src_b = bf16[8,192,128]{2,1,0:T(8,128)(2,1)S(1)} collective-permute-done((bf16[8,192,128]{2,1,0:T(8,128)(2,1)}, bf16[8,192,128]{2,1,0:T(8,128)(2,1)S(1)}, u32[]{:S(2)}, u32[]{:S(2)}) %collective-permute-start.2) | collective-permute-done | bytes 393248 | tf_op jit(solution)/shard_map/ppermute | solution.py:389
  127.8 1.7 collective-permute-done.3.src_c
  130.3 10.2 %shard_map.83 = (bf16[16,192,128]{2,1,0:T(8,128)(2,1)}, bf16[18,192,128]{2,1,0:T(8,128)(2,1)}) custom-call(s32[5,4]{1,0:T(8,128)} %add_add_fusion.flags, bf16[3,16,192,128]{3,2,1,0:T(8,128)(2,1)} %all-gather.5.cloned.1.call-done.caches.frames, bf16[18,192,128]{2,1,0:T(8,128)(2,1)} %get-tuple-element.39.a_p.a_pp, ...), custom_call_target="tpu_custom_call" | custom-call | tf_op jit(solution)/shard_map/pallas_call | solution.py:286
  140.6 6.9 %shard_map.84 = (bf16[8,192,128]{2,1,0:T(8,128)(2,1)}, bf16[18,192,128]{2,1,0:T(8,128)(2,1)}) custom-call(s32[5,4]{1,0:T(8,128)} %add_add_fusion.flags, bf16[2,16,192,128]{3,2,1,0:T(8,128)(2,1)} %bitcast.115, bf16[18,192,128]{2,1,0:T(8,128)(2,1)} %get-tuple-element.36.rest_0_.a_p.a_pp, bf16[18,192,128]{2,1,0:T(8,128)(2,1)} %get-tuple-element.31.rest_0_.a_p.a_pp, ...), custom_call_target="tpu_custom_call" | custom-call | tf_op jit(solution)/shard_map/pallas_call | solution.py:286
  147.4 2.7 %collective-permute-start.4 = (bf16[8,192,128]{2,1,0:T(8,128)(2,1)}, bf16[8,192,128]{2,1,0:T(8,128)(2,1)S(1)}, u32[]{:S(2)}, u32[]{:S(2)}) collective-permute-start(bf16[8,192,128]{2,1,0:T(8,128)(2,1)} %get-tuple-element.42), channel_id=1, source_target_pairs={{0,8},{8,16},{16,24},{1,9},{9,17},{17,25},{2,10},{10,18},{18,26},{... | collective-permute-start | bytes 1179656 | tf_op jit(solution)/shard_map/ppermute | solution.py:389
  150.1 6.9 %shard_map.85 = bf16[8,192,128]{2,1,0:T(8,128)(2,1)} custom-call(s32[5,4]{1,0:T(8,128)} %add_add_fusion.flags, bf16[2,16,192,128]{3,2,1,0:T(8,128)(2,1)} %bitcast.116, bf16[18,192,128]{2,1,0:T(8,128)(2,1)} %get-tuple-element.36.rest_0_.a_p.a_pp, bf16[18,192,128]{2,1,0:T(8,128)(2,1)} %get-tuple-element.31.rest_0_.a_p.a_pp, ...), custom_call_target="tpu_custom_call" | custom-call | tf_op jit(solution)/shard_map/pallas_call | solution.py:286
  157.0 4.6 %collective-permute-done.4.src_b = bf16[8,192,128]{2,1,0:T(8,128)(2,1)S(1)} collective-permute-done((bf16[8,192,128]{2,1,0:T(8,128)(2,1)}, bf16[8,192,128]{2,1,0:T(8,128)(2,1)S(1)}, u32[]{:S(2)}, u32[]{:S(2)}) %collective-permute-start.4) | collective-permute-done | bytes 393248 | tf_op jit(solution)/shard_map/ppermute | solution.py:389
  161.6 1.7 collective-permute-done.5.src_c
  164.1 10.3 %shard_map.86 = (bf16[16,192,128]{2,1,0:T(8,128)(2,1)}, bf16[18,192,128]{2,1,0:T(8,128)(2,1)}) custom-call(s32[5,4]{1,0:T(8,128)} %add_add_fusion.flags, bf16[3,16,192,128]{3,2,1,0:T(8,128)(2,1)} %all-gather.5.cloned.1.call-done.caches.frames, bf16[18,192,128]{2,1,0:T(8,128)(2,1)} %get-tuple-element.44.a_p.a_pp, ...), custom_call_target="tpu_custom_call" | custom-call | tf_op jit(solution)/shard_map/pallas_call | solution.py:286
  174.4 6.9 %shard_map.87 = (bf16[8,192,128]{2,1,0:T(8,128)(2,1)}, bf16[18,192,128]{2,1,0:T(8,128)(2,1)}) custom-call(s32[5,4]{1,0:T(8,128)} %add_add_fusion.flags, bf16[2,16,192,128]{3,2,1,0:T(8,128)(2,1)} %bitcast.117, bf16[18,192,128]{2,1,0:T(8,128)(2,1)} %get-tuple-element.41.rest_0_.a_p.a_pp, bf16[18,192,128]{2,1,0:T(8,128)(2,1)} %get-tuple-element.36.rest_0_.a_p.a_pp, ...), custom_call_target="tpu_custom_call" | custom-call | tf_op jit(solution)/shard_map/pallas_call | solution.py:286
  181.2 2.1 collective-permute-start.6
  183.4 7.0 %shard_map.88 = bf16[8,192,128]{2,1,0:T(8,128)(2,1)} custom-call(s32[5,4]{1,0:T(8,128)} %add_add_fusion.flags, bf16[2,16,192,128]{3,2,1,0:T(8,128)(2,1)} %bitcast.118, bf16[18,192,128]{2,1,0:T(8,128)(2,1)} %get-tuple-element.41.rest_0_.a_p.a_pp, bf16[18,192,128]{2,1,0:T(8,128)(2,1)} %get-tuple-element.36.rest_0_.a_p.a_pp, ...), custom_call_target="tpu_custom_call" | custom-call | tf_op jit(solution)/shard_map/pallas_call | solution.py:286
  190.4 5.0 %collective-permute-done.6.src_b = bf16[8,192,128]{2,1,0:T(8,128)(2,1)S(1)} collective-permute-done((bf16[8,192,128]{2,1,0:T(8,128)(2,1)}, bf16[8,192,128]{2,1,0:T(8,128)(2,1)S(1)}, u32[]{:S(2)}, u32[]{:S(2)}) %collective-permute-start.6) | collective-permute-done | bytes 393248 | tf_op jit(solution)/shard_map/ppermute | solution.py:389
  195.4 1.0 slice.52
  196.4 1.2 select_bitcast_fusion.3
  198.4 10.3 %shard_map.89 = (bf16[16,192,128]{2,1,0:T(8,128)(2,1)}, bf16[18,192,128]{2,1,0:T(8,128)(2,1)}) custom-call(s32[5,4]{1,0:T(8,128)} %add_add_fusion.flags, bf16[3,16,192,128]{3,2,1,0:T(8,128)(2,1)} %all-gather.5.cloned.1.call-done.caches.frames, bf16[18,192,128]{2,1,0:T(8,128)(2,1)} %get-tuple-element.53.a_p, ...), custom_call_target="tpu_custom_call" | custom-call | tf_op jit(solution)/shard_map/pallas_call | solution.py:286
  208.8 1.1 fusion.7
  209.9 9.2 %shard_map.90 = (bf16[16,192,128]{2,1,0:T(8,128)(2,1)}, bf16[18,192,128]{2,1,0:T(8,128)(2,1)}) custom-call(s32[5,4]{1,0:T(8,128)} %add_add_fusion.flags, bf16[2,16,192,128]{3,2,1,0:T(8,128)(2,1)} %bitcast.119, bf16[18,192,128]{2,1,0:T(8,128)(2,1)} %get-tuple-element.47.rest_0_.a_p, bf16[18,192,128]{2,1,0:T(8,128)(2,1)} %get-tuple-element.41.rest_0_.a_p.a_pp, ...), custom_call_target="tpu_custom_call" | custom-call | tf_op jit(solution)/shard_map/pallas_call | solution.py:286
  219.1 1.2 fusion.1
  220.4 1.2 copy.61
  221.5 1.2 select_bitcast_fusion.2
  222.8 0.9 copy.60
  (61 shorter events, 9.1 us)
Async XLA Ops:
  7.2 35.9 %all-gather.5.cloned.1.call-start = ((), (), s32[]{:S(2)}) async-start(), calls=%async_computation | async-start | bytes 2654208 | tf_op jit(solution)/shard_map/all_gather | solution.py:342
  10.0 59.4 %all-gather.9.cloned.1.call-start = ((), (), s32[]{:S(2)}) async-start(), calls=%async_computation.2 | async-start | bytes 1769472 | tf_op jit(solution)/shard_map/all_gather | solution.py:343
  10.8 84.9 %all-gather.7.cloned.1.call-start = ((), (), s32[]{:S(2)}) async-start(), calls=%async_computation.1 | async-start | bytes 1769472 | tf_op jit(solution)/shard_map/all_gather | solution.py:347
  19.8 4.4 %copy-start.10 = (f32[1,2,192]{2,1,0:T(2,128)S(1)}, f32[1,2,192]{2,1,0:T(2,128)}, u32[]{:S(2)}) copy-start(f32[1,2,192]{2,1,0:T(2,128)} %param.9) | copy-start | bytes 4612
  19.8 5.2 %copy-start.11 = (f32[1,2,192]{2,1,0:T(2,128)S(1)}, f32[1,2,192]{2,1,0:T(2,128)}, u32[]{:S(2)}) copy-start(f32[1,2,192]{2,1,0:T(2,128)} %param.10) | copy-start | bytes 4612
  19.8 6.0 %copy-start.12 = (f32[1,2,192]{2,1,0:T(2,128)S(1)}, f32[1,2,192]{2,1,0:T(2,128)}, u32[]{:S(2)}) copy-start(f32[1,2,192]{2,1,0:T(2,128)} %param.11) | copy-start | bytes 4612
  30.6 6.6 %copy-start.13 = (s32[4]{0:T(128)S(1)}, s32[4]{0:T(128)}, u32[]{:S(2)}) copy-start(s32[4]{0:T(128)} %pad.15.clone) | copy-start | bytes 52
  76.3 14.3 %collective-permute-start = (bf16[8,192,128]{2,1,0:T(8,128)(2,1)}, bf16[8,192,128]{2,1,0:T(8,128)(2,1)S(1)}, u32[]{:S(2)}, u32[]{:S(2)}) collective-permute-start(bf16[8,192,128]{2,1,0:T(8,128)(2,1)} %get-tuple-element.32), channel_id=1, source_target_pairs={{0,8},{8,16},{16,24},{1,9},{9,17},{17,25},{2,10},{10,18},{18,26},{... | collective-permute-start | bytes 1179656 | tf_op jit(solution)/shard_map/ppermute | solution.py:389
  90.6 5.1 %copy-start.1 = (bf16[8,192,128]{2,1,0:T(8,128)(2,1)}, bf16[8,192,128]{2,1,0:T(8,128)(2,1)S(1)}, u32[]{:S(2)}) copy-start(bf16[8,192,128]{2,1,0:T(8,128)(2,1)S(1)} %collective-permute-done.src_b) | copy-start | bytes 1179652
  90.6 5.1 %collective-permute-start.1 = (bf16[8,192,128]{2,1,0:T(8,128)(2,1)S(1)}, bf16[8,192,128]{2,1,0:T(8,128)(2,1)S(1)}, u32[]{:S(2)}, u32[]{:S(2)}) collective-permute-start(bf16[8,192,128]{2,1,0:T(8,128)(2,1)S(1)} %collective-permute-done.src_b), channel_id=1, source_target_pairs={{0,1},{1,0},{2,3},{3,2},{4,5},{5,4},{6,7},{7,6},{8,9},{9,8},{10,11... | collective-permute-start | bytes 1179656 | tf_op jit(solution)/shard_map/ppermute | solution.py:391
  95.7 0.8 copy-start.4
  113.6 14.3 %collective-permute-start.2 = (bf16[8,192,128]{2,1,0:T(8,128)(2,1)}, bf16[8,192,128]{2,1,0:T(8,128)(2,1)S(1)}, u32[]{:S(2)}, u32[]{:S(2)}) collective-permute-start(bf16[8,192,128]{2,1,0:T(8,128)(2,1)} %get-tuple-element.37), channel_id=1, source_target_pairs={{0,8},{8,16},{16,24},{1,9},{9,17},{17,25},{2,10},{10,18},{18,26},{... | collective-permute-start | bytes 1179656 | tf_op jit(solution)/shard_map/ppermute | solution.py:389
  127.8 1.7 copy-start.2
  127.8 1.7 collective-permute-start.3
  129.6 0.7 copy-start.5
  147.4 14.2 %collective-permute-start.4 = (bf16[8,192,128]{2,1,0:T(8,128)(2,1)}, bf16[8,192,128]{2,1,0:T(8,128)(2,1)S(1)}, u32[]{:S(2)}, u32[]{:S(2)}) collective-permute-start(bf16[8,192,128]{2,1,0:T(8,128)(2,1)} %get-tuple-element.42), channel_id=1, source_target_pairs={{0,8},{8,16},{16,24},{1,9},{9,17},{17,25},{2,10},{10,18},{18,26},{... | collective-permute-start | bytes 1179656 | tf_op jit(solution)/shard_map/ppermute | solution.py:389
  161.6 1.7 copy-start.3
  161.6 1.7 collective-permute-start.5
  163.3 0.7 copy-start.6
  181.2 14.2 %collective-permute-start.6 = (bf16[8,192,128]{2,1,0:T(8,128)(2,1)}, bf16[8,192,128]{2,1,0:T(8,128)(2,1)S(1)}, u32[]{:S(2)}, u32[]{:S(2)}) collective-permute-start(bf16[8,192,128]{2,1,0:T(8,128)(2,1)} %get-tuple-element.46), channel_id=1, source_target_pairs={{0,8},{8,16},{16,24},{1,9},{9,17},{17,25},{2,10},{10,18},{18,26},{... | collective-permute-start | bytes 1179656 | tf_op jit(solution)/shard_map/ppermute | solution.py:389
  183.4 12.0 %copy-start = (bf16[1,2,16,192,128]{4,3,2,1,0:T(8,128)(2,1)S(1)}, bf16[1,2,16,192,128]{4,3,2,1,0:T(8,128)(2,1)}, u32[]{:S(2)}) copy-start(bf16[1,2,16,192,128]{4,3,2,1,0:T(8,128)(2,1)} %all-gather.9.cloned.1.call-done) | copy-start | bytes 4718596
  190.4 6.0 %copy-start.9 = (bf16[8,192,128]{2,1,0:T(8,128)(2,1)S(1)}, bf16[8,192,128]{2,1,0:T(8,128)(2,1)}, u32[]{:S(2)}) copy-start(bf16[8,192,128]{2,1,0:T(8,128)(2,1)} %shard_map.82) | copy-start | bytes 1179652
  195.4 2.3 copy-start.7
  195.4 2.2 collective-permute-start.7
  197.6 0.8 copy-start.8
  198.4 10.3 %slice-start = ((bf16[3,16,192,128]{3,2,1,0:T(8,128)(2,1)}), bf16[1,16,192,128]{3,2,1,0:T(8,128)(2,1)S(1)}, s32[]{:S(2)}) async-start(bf16[3,16,192,128]{3,2,1,0:T(8,128)(2,1)} %all-gather.5.cloned.1.call-done.caches.frames), calls=%async_computation.3 | async-start | bytes 1572864 | tf_op jit(solution)/shard_map/slice | solution.py:395
Sparse Core Ops, SparseCore 0:
  10.2 32.8 all-gather.4
  45.2 24.1 all-gather.8
  71.0 24.5 all-gather.6
where the time goes:
time: 235 us; the launch traced here: 230 us
  Pallas kernels  116 us (49%)
  waiting for transfers between devices  42.9 us (18%)
  local copies, waits for them, and re-layouts  36.3 us (15%)
  between operations  14.3 us (6%)
  starting transfers between devices  12.3 us (5%)
  other arithmetic  8.39 us (4%)
    pallas_call x14, Pallas kernels, fused_conv(): pl.pallas_call(body, out_shape=shapes, in_specs=specs, out_specs=vmem if...  116 us
    ppermute x4, waiting for transfers between devices, shards_whole(): got = lax.ppermute(lead, 'phase', forward)  16.8 us
    all_gather x1, waiting for transfers between devices, shards_whole(): second_cache = lax.all_gather(cache_t[1], 'rows', axis=1, tiled=True)  13.8 us
    ppermute x4, starting transfers between devices, shards_whole(): got = lax.ppermute(lead, 'phase', forward)  12.2 us
    transpose x3, local copies, waits for them, and re-layouts, arrange_taps(): jnp.transpose(weight, (2, 3, 0, 1, 4)).reshape(3 * outputs, 9 * channels)  11 us
    reshape x2, local copies, waits for them, and re-layouts, arrange_taps(): jnp.transpose(weight, (2, 3, 0, 1, 4)).reshape(3 * outputs, 9 * channels)  8.65 us
    unnamed x32, local copies, waits for them, and re-layouts  7.07 us
    all_gather x1, waiting for transfers between devices, shards_whole(): lax.all_gather(jnp.stack(later), 'rows', axis=1, tiled=True)  5.08 us
  transfers between devices with their start and end apart: 11, of which 9 were waited for; matrix products, arithmetic and copies ran while one was open for 14% of the time, Pallas kernels for 20%

commit v1 on v0

--- a/solution.py
+++ b/solution.py
@@ -190,17 +190,33 @@
 
     pltpu.make_async_copy(taps, tapbuf, sems.at[4]).start()
 
-    @pl.when(mode == 0)
-    def _():
-        begin([(whole.at[pl.ds(0, half)], top), (whole.at[pl.ds(half, half)], bottom)], 0)
-
-    @pl.when(mode == 1)
-    def _():
-        begin([(src_b, top), (src_c, bottom)], 0)
-
-    @pl.when(mode == 2)
-    def _():
-        begin([(src_c, top), (src_b, bottom)], 0)
+    if kind in ("lead", "tail"):
+        part = core * half if kind == "lead" else (1 - core) * half
+        mine = rawbuf.at[pl.ds(part, half)]
+        source_copies = [(src_b, mine)]
+
+        @pl.when(mode == 0)
+        def _():
+            begin([(whole.at[pl.ds(part, half)], mine)], 0)
+
+        @pl.when(mode != 0)
+        def _():
+            begin([(src_b if kind == "lead" else src_c, mine)], 0)
+
+    else:
+        source_copies = [(src_b, top), (src_c, bottom)]
+
+        @pl.when(mode == 0)
+        def _():
+            begin([(whole.at[pl.ds(0, half)], top), (whole.at[pl.ds(half, half)], bottom)], 0)
+
+        @pl.when(mode == 1)
+        def _():
+            begin([(src_b, top), (src_c, bottom)], 0)
+
+        @pl.when(mode == 2)
+        def _():
+            begin([(src_c, top), (src_b, bottom)], 0)
 
     @pl.when(first == 1)
     def _():
@@ -218,7 +234,6 @@
     for x in (x0, x1):
         x[0] = zero
         x[span + 1] = zero
-    source_copies = [(src_b, top), (src_c, bottom)]
     history_copies = [(inner(a_pp), inner0), (inner(a_p), inner1)]
 
     if kind != "tail":

time: 235 us -> 235 us (level)
  transfers between devices with their start and end apart: 11 -> 11, of which waited for: 9 -> 9; matrix products, arithmetic and copies ran while one was open for 14% -> 14% of each run, Pallas kernels for 20% -> 19%
where the time goes in v1:
time: 235 us; the launch traced here: 230 us
  Pallas kernels  115 us (49%)
  waiting for transfers between devices  43.6 us (19%)
  local copies, waits for them, and re-layouts  36.3 us (15%)
  between operations  14.3 us (6%)
  starting transfers between devices  12.3 us (5%)
  other arithmetic  8.39 us (4%)
    pallas_call x14, Pallas kernels, fused_conv(): pl.pallas_call(body, out_shape=shapes, in_specs=specs, out_specs=vmem if...  115 us
    ppermute x4, waiting for transfers between devices, shards_whole(): got = lax.ppermute(lead, 'phase', forward)  17.3 us
    all_gather x1, waiting for transfers between devices, shards_whole(): second_cache = lax.all_gather(cache_t[1], 'rows', axis=1, tiled=True)  13.8 us
    ppermute x4, starting transfers between devices, shards_whole(): got = lax.ppermute(lead, 'phase', forward)  12.2 us
    transpose x3, local copies, waits for them, and re-layouts, arrange_taps(): jnp.transpose(weight, (2, 3, 0, 1, 4)).reshape(3 * outputs, 9 * channels)  11 us
    reshape x2, local copies, waits for them, and re-layouts, arrange_taps(): jnp.transpose(weight, (2, 3, 0, 1, 4)).reshape(3 * outputs, 9 * channels)  8.65 us
    unnamed x32, local copies, waits for them, and re-layouts  7.07 us
    all_gather x1, waiting for transfers between devices, shards_whole(): lax.all_gather(jnp.stack(later), 'rows', axis=1, tiled=True)  5.2 us
  transfers between devices with their start and end apart: 11, of which 9 were waited for; matrix products, arithmetic and copies ran while one was open for 14% of the time, Pallas kernels for 19%

profile of v1, /device:TPU:4, one launch (start us, length us, event | category | flops | bytes accessed | tf_op | source)
XLA Modules:
  0.0 230.1 jit_solution(1744901755958201957)
XLA Ops:
  7.2 1.0 copy.64
  8.3 1.0 copy.65
  12.8 4.7 %slice_bitcast_fusion = (bf16[3,192,3,3,192]{4,1,0,3,2:T(8,128)(2,1)S(1)}, bf16[3,192,3,3,192]{4,1,0,3,2:T(8,128)(2,1)}) fusion(bf16[1,2,3,3,3,192,192]{6,5,4,3,2,1,0:T(8,128)(2,1)} %param.8), kind=kLoop, calls=%fused_computation | loop fusion | bytes 7962624 | tf_op jit(solution)/shard_map/transpose | solution.py:77
  17.5 2.3 copy.17
  19.8 4.4 %reshape.59.taps = bf16[576,1728]{1,0:T(8,128)(2,1)} reshape(bf16[3,192,3,3,192]{4,3,2,1,0:T(4,128)(2,1)S(1)} %copy.17) | data formatting | bytes 3981312 | tf_op jit(solution)/shard_map/reshape | solution.py:77
  24.2 0.8 copy.18.bias
  25.0 0.8 copy.19.gain
  26.5 4.1 %copy.16 = bf16[3,192,3,3,192]{4,3,2,1,0:T(4,128)(2,1)S(1)} copy(bf16[3,192,3,3,192]{4,1,0,3,2:T(8,128)(2,1)} %get-tuple-element.63) | data formatting | bytes 3981312 | tf_op jit(solution)/shard_map/transpose | solution.py:77
  30.6 4.2 %reshape.58.taps = bf16[576,1728]{1,0:T(8,128)(2,1)} reshape(bf16[3,192,3,3,192]{4,3,2,1,0:T(4,128)(2,1)S(1)} %copy.16) | data formatting | bytes 3981312 | tf_op jit(solution)/shard_map/reshape | solution.py:77
  34.9 0.8 copy.21.bias
  37.2 1.3 add_add_fusion.flags
  38.5 0.8 compare_convert_fusion.member
  39.3 3.8 %all-gather.5.cloned.1.call-done.caches.frames = bf16[3,16,192,128]{3,2,1,0:T(8,128)(2,1)} async-done(((bf16[3,2,192,128]{3,2,1,0:T(8,128)(2,1)}), bf16[3,16,192,128]{3,2,1,0:T(8,128)(2,1)}) %all-gather.5.cloned.1.call-update) | async-done | bytes 2359312 | tf_op jit(solution)/shard_map/all_gather | solution.py:357
  43.0 1.2 broadcast_in_dim.8.a_p.a_pp
  44.2 0.8 broadcast_in_dim.9.src_b.src_c
  45.0 10.7 %shard_map.77 = (bf16[16,192,128]{2,1,0:T(8,128)(2,1)}, bf16[18,192,128]{2,1,0:T(8,128)(2,1)}) custom-call(s32[5,4]{1,0:T(8,128)} %add_add_fusion.flags, bf16[3,16,192,128]{3,2,1,0:T(8,128)(2,1)} %all-gather.5.cloned.1.call-done.caches.frames, bf16[18,192,128]{2,1,0:T(8,128)(2,1)} %broadcast_in_dim.8.a_p.a_pp, ...), custom_call_target="tpu_custom_call" | custom-call | tf_op jit(solution)/shard_map/pallas_call | solution.py:301
  55.7 13.8 %all-gather.9.cloned.1.call-done = bf16[1,2,16,192,128]{4,3,2,1,0:T(8,128)(2,1)} async-done(((bf16[1,2,2,192,128]{4,3,2,1,0:T(8,128)(2,1)}), bf16[1,2,16,192,128]{4,3,2,1,0:T(8,128)(2,1)}) %all-gather.9.cloned.1.call-update) | async-done | bytes 1572880 | tf_op jit(solution)/shard_map/all_gather | solution.py:358
  69.4 6.8 %shard_map.78 = (bf16[8,192,128]{2,1,0:T(8,128)(2,1)}, bf16[18,192,128]{2,1,0:T(8,128)(2,1)}) custom-call(s32[5,4]{1,0:T(8,128)} %add_add_fusion.flags, bf16[2,16,192,128]{3,2,1,0:T(8,128)(2,1)} %bitcast.111, bf16[18,192,128]{2,1,0:T(8,128)(2,1)} %broadcast_in_dim.8.a_p.a_pp, bf16[18,192,128]{2,1,0:T(8,128)(2,1)} %broadcast_in_dim.8.a_p.a_pp, ...), custom_call_target="tpu_custom_call" | custom-call | tf_op jit(solution)/shard_map/pallas_call | solution.py:301
  76.2 3.6 %collective-permute-start = (bf16[8,192,128]{2,1,0:T(8,128)(2,1)}, bf16[8,192,128]{2,1,0:T(8,128)(2,1)S(1)}, u32[]{:S(2)}, u32[]{:S(2)}) collective-permute-start(bf16[8,192,128]{2,1,0:T(8,128)(2,1)} %get-tuple-element.32), channel_id=1, source_target_pairs={{0,8},{8,16},{16,24},{1,9},{9,17},{17,25},{2,10},{10,18},{18,26},{... | collective-permute-start | bytes 1179656 | tf_op jit(solution)/shard_map/ppermute | solution.py:404
  79.8 6.8 %shard_map.79 = bf16[8,192,128]{2,1,0:T(8,128)(2,1)} custom-call(s32[5,4]{1,0:T(8,128)} %add_add_fusion.flags, bf16[2,16,192,128]{3,2,1,0:T(8,128)(2,1)} %bitcast.112, bf16[18,192,128]{2,1,0:T(8,128)(2,1)} %broadcast_in_dim.8.a_p.a_pp, bf16[18,192,128]{2,1,0:T(8,128)(2,1)} %broadcast_in_dim.8.a_p.a_pp, ...), custom_call_target="tpu_custom_call" | custom-call | tf_op jit(solution)/shard_map/pallas_call | solution.py:301
  86.6 3.8 %collective-permute-done.src_b = bf16[8,192,128]{2,1,0:T(8,128)(2,1)S(1)} collective-permute-done((bf16[8,192,128]{2,1,0:T(8,128)(2,1)}, bf16[8,192,128]{2,1,0:T(8,128)(2,1)S(1)}, u32[]{:S(2)}, u32[]{:S(2)}) %collective-permute-start) | collective-permute-done | bytes 393248 | tf_op jit(solution)/shard_map/ppermute | solution.py:404
  90.5 5.2 %all-gather.7.cloned.1.call-done.frames = bf16[2,16,192,128]{3,2,1,0:T(8,128)(2,1)} async-done(((bf16[2,2,192,128]{3,2,1,0:T(8,128)(2,1)}), bf16[2,16,192,128]{3,2,1,0:T(8,128)(2,1)}) %all-gather.7.cloned.1.call-update) | async-done | bytes 1572880 | tf_op jit(solution)/shard_map/all_gather | solution.py:362
  96.4 10.2 %shard_map.80 = (bf16[16,192,128]{2,1,0:T(8,128)(2,1)}, bf16[18,192,128]{2,1,0:T(8,128)(2,1)}) custom-call(s32[5,4]{1,0:T(8,128)} %add_add_fusion.flags, bf16[3,16,192,128]{3,2,1,0:T(8,128)(2,1)} %all-gather.5.cloned.1.call-done.caches.frames, bf16[18,192,128]{2,1,0:T(8,128)(2,1)} %get-tuple-element.34.a_p.a_pp, ...), custom_call_target="tpu_custom_call" | custom-call | tf_op jit(solution)/shard_map/pallas_call | solution.py:301
  106.7 6.8 %shard_map.81 = (bf16[8,192,128]{2,1,0:T(8,128)(2,1)}, bf16[18,192,128]{2,1,0:T(8,128)(2,1)}) custom-call(s32[5,4]{1,0:T(8,128)} %add_add_fusion.flags, bf16[2,16,192,128]{3,2,1,0:T(8,128)(2,1)} %bitcast.113, bf16[18,192,128]{2,1,0:T(8,128)(2,1)} %get-tuple-element.31.rest_0_.a_p.a_pp, bf16[18,192,128]{2,1,0:T(8,128)(2,1)} %broadcast_in_dim.8.a_p.a_pp, ...), custom_call_target="tpu_custom_call" | custom-call | tf_op jit(solution)/shard_map/pallas_call | solution.py:301
  113.5 3.8 %collective-permute-start.2 = (bf16[8,192,128]{2,1,0:T(8,128)(2,1)}, bf16[8,192,128]{2,1,0:T(8,128)(2,1)S(1)}, u32[]{:S(2)}, u32[]{:S(2)}) collective-permute-start(bf16[8,192,128]{2,1,0:T(8,128)(2,1)} %get-tuple-element.37), channel_id=1, source_target_pairs={{0,8},{8,16},{16,24},{1,9},{9,17},{17,25},{2,10},{10,18},{18,26},{... | collective-permute-start | bytes 1179656 | tf_op jit(solution)/shard_map/ppermute | solution.py:404
  117.3 6.8 %shard_map.82 = bf16[8,192,128]{2,1,0:T(8,128)(2,1)} custom-call(s32[5,4]{1,0:T(8,128)} %add_add_fusion.flags, bf16[2,16,192,128]{3,2,1,0:T(8,128)(2,1)} %bitcast.114, bf16[18,192,128]{2,1,0:T(8,128)(2,1)} %get-tuple-element.31.rest_0_.a_p.a_pp, bf16[18,192,128]{2,1,0:T(8,128)(2,1)} %broadcast_in_dim.8.a_p.a_pp, ...), custom_call_target="tpu_custom_call" | custom-call | tf_op jit(solution)/shard_map/pallas_call | solution.py:301
  124.1 3.6 %collective-permute-done.2.src_b = bf16[8,192,128]{2,1,0:T(8,128)(2,1)S(1)} collective-permute-done((bf16[8,192,128]{2,1,0:T(8,128)(2,1)}, bf16[8,192,128]{2,1,0:T(8,128)(2,1)S(1)}, u32[]{:S(2)}, u32[]{:S(2)}) %collective-permute-start.2) | collective-permute-done | bytes 393248 | tf_op jit(solution)/shard_map/ppermute | solution.py:404
  127.7 1.7 collective-permute-done.3.src_c
  130.2 10.2 %shard_map.83 = (bf16[16,192,128]{2,1,0:T(8,128)(2,1)}, bf16[18,192,128]{2,1,0:T(8,128)(2,1)}) custom-call(s32[5,4]{1,0:T(8,128)} %add_add_fusion.flags, bf16[3,16,192,128]{3,2,1,0:T(8,128)(2,1)} %all-gather.5.cloned.1.call-done.caches.frames, bf16[18,192,128]{2,1,0:T(8,128)(2,1)} %get-tuple-element.39.a_p.a_pp, ...), custom_call_target="tpu_custom_call" | custom-call | tf_op jit(solution)/shard_map/pallas_call | solution.py:301
  140.4 6.8 %shard_map.84 = (bf16[8,192,128]{2,1,0:T(8,128)(2,1)}, bf16[18,192,128]{2,1,0:T(8,128)(2,1)}) custom-call(s32[5,4]{1,0:T(8,128)} %add_add_fusion.flags, bf16[2,16,192,128]{3,2,1,0:T(8,128)(2,1)} %bitcast.115, bf16[18,192,128]{2,1,0:T(8,128)(2,1)} %get-tuple-element.36.rest_0_.a_p.a_pp, bf16[18,192,128]{2,1,0:T(8,128)(2,1)} %get-tuple-element.31.rest_0_.a_p.a_pp, ...), custom_call_target="tpu_custom_call" | custom-call | tf_op jit(solution)/shard_map/pallas_call | solution.py:301
  147.2 2.7 %collective-permute-start.4 = (bf16[8,192,128]{2,1,0:T(8,128)(2,1)}, bf16[8,192,128]{2,1,0:T(8,128)(2,1)S(1)}, u32[]{:S(2)}, u32[]{:S(2)}) collective-permute-start(bf16[8,192,128]{2,1,0:T(8,128)(2,1)} %get-tuple-element.42), channel_id=1, source_target_pairs={{0,8},{8,16},{16,24},{1,9},{9,17},{17,25},{2,10},{10,18},{18,26},{... | collective-permute-start | bytes 1179656 | tf_op jit(solution)/shard_map/ppermute | solution.py:404
  149.9 6.8 %shard_map.85 = bf16[8,192,128]{2,1,0:T(8,128)(2,1)} custom-call(s32[5,4]{1,0:T(8,128)} %add_add_fusion.flags, bf16[2,16,192,128]{3,2,1,0:T(8,128)(2,1)} %bitcast.116, bf16[18,192,128]{2,1,0:T(8,128)(2,1)} %get-tuple-element.36.rest_0_.a_p.a_pp, bf16[18,192,128]{2,1,0:T(8,128)(2,1)} %get-tuple-element.31.rest_0_.a_p.a_pp, ...), custom_call_target="tpu_custom_call" | custom-call | tf_op jit(solution)/shard_map/pallas_call | solution.py:301
  156.7 4.7 %collective-permute-done.4.src_b = bf16[8,192,128]{2,1,0:T(8,128)(2,1)S(1)} collective-permute-done((bf16[8,192,128]{2,1,0:T(8,128)(2,1)}, bf16[8,192,128]{2,1,0:T(8,128)(2,1)S(1)}, u32[]{:S(2)}, u32[]{:S(2)}) %collective-permute-start.4) | collective-permute-done | bytes 393248 | tf_op jit(solution)/shard_map/ppermute | solution.py:404
  161.4 1.7 collective-permute-done.5.src_c
  163.8 10.3 %shard_map.86 = (bf16[16,192,128]{2,1,0:T(8,128)(2,1)}, bf16[18,192,128]{2,1,0:T(8,128)(2,1)}) custom-call(s32[5,4]{1,0:T(8,128)} %add_add_fusion.flags, bf16[3,16,192,128]{3,2,1,0:T(8,128)(2,1)} %all-gather.5.cloned.1.call-done.caches.frames, bf16[18,192,128]{2,1,0:T(8,128)(2,1)} %get-tuple-element.44.a_p.a_pp, ...), custom_call_target="tpu_custom_call" | custom-call | tf_op jit(solution)/shard_map/pallas_call | solution.py:301
  174.1 6.8 %shard_map.87 = (bf16[8,192,128]{2,1,0:T(8,128)(2,1)}, bf16[18,192,128]{2,1,0:T(8,128)(2,1)}) custom-call(s32[5,4]{1,0:T(8,128)} %add_add_fusion.flags, bf16[2,16,192,128]{3,2,1,0:T(8,128)(2,1)} %bitcast.117, bf16[18,192,128]{2,1,0:T(8,128)(2,1)} %get-tuple-element.41.rest_0_.a_p.a_pp, bf16[18,192,128]{2,1,0:T(8,128)(2,1)} %get-tuple-element.36.rest_0_.a_p.a_pp, ...), custom_call_target="tpu_custom_call" | custom-call | tf_op jit(solution)/shard_map/pallas_call | solution.py:301
  180.9 2.1 collective-permute-start.6
  183.0 6.9 %shard_map.88 = bf16[8,192,128]{2,1,0:T(8,128)(2,1)} custom-call(s32[5,4]{1,0:T(8,128)} %add_add_fusion.flags, bf16[2,16,192,128]{3,2,1,0:T(8,128)(2,1)} %bitcast.118, bf16[18,192,128]{2,1,0:T(8,128)(2,1)} %get-tuple-element.41.rest_0_.a_p.a_pp, bf16[18,192,128]{2,1,0:T(8,128)(2,1)} %get-tuple-element.36.rest_0_.a_p.a_pp, ...), custom_call_target="tpu_custom_call" | custom-call | tf_op jit(solution)/shard_map/pallas_call | solution.py:301
  189.9 5.1 %collective-permute-done.6.src_b = bf16[8,192,128]{2,1,0:T(8,128)(2,1)S(1)} collective-permute-done((bf16[8,192,128]{2,1,0:T(8,128)(2,1)}, bf16[8,192,128]{2,1,0:T(8,128)(2,1)S(1)}, u32[]{:S(2)}, u32[]{:S(2)}) %collective-permute-start.6) | collective-permute-done | bytes 393248 | tf_op jit(solution)/shard_map/ppermute | solution.py:404
  195.1 1.0 slice.52
  196.1 1.2 select_bitcast_fusion.3
  198.1 10.3 %shard_map.89 = (bf16[16,192,128]{2,1,0:T(8,128)(2,1)}, bf16[18,192,128]{2,1,0:T(8,128)(2,1)}) custom-call(s32[5,4]{1,0:T(8,128)} %add_add_fusion.flags, bf16[3,16,192,128]{3,2,1,0:T(8,128)(2,1)} %all-gather.5.cloned.1.call-done.caches.frames, bf16[18,192,128]{2,1,0:T(8,128)(2,1)} %get-tuple-element.53.a_p, ...), custom_call_target="tpu_custom_call" | custom-call | tf_op jit(solution)/shard_map/pallas_call | solution.py:301
  208.4 1.1 fusion.7
  209.6 9.2 %shard_map.90 = (bf16[16,192,128]{2,1,0:T(8,128)(2,1)}, bf16[18,192,128]{2,1,0:T(8,128)(2,1)}) custom-call(s32[5,4]{1,0:T(8,128)} %add_add_fusion.flags, bf16[2,16,192,128]{3,2,1,0:T(8,128)(2,1)} %bitcast.119, bf16[18,192,128]{2,1,0:T(8,128)(2,1)} %get-tuple-element.47.rest_0_.a_p, bf16[18,192,128]{2,1,0:T(8,128)(2,1)} %get-tuple-element.41.rest_0_.a_p.a_pp, ...), custom_call_target="tpu_custom_call" | custom-call | tf_op jit(solution)/shard_map/pallas_call | solution.py:301
  218.8 1.2 fusion.1
  220.0 1.2 copy.61
  221.2 1.2 select_bitcast_fusion.2
  222.4 0.9 copy.60
  (61 shorter events, 9.1 us)
Async XLA Ops:
  7.2 35.9 %all-gather.5.cloned.1.call-start = ((), (), s32[]{:S(2)}) async-start(), calls=%async_computation | async-start | bytes 2654208 | tf_op jit(solution)/shard_map/all_gather | solution.py:357
  10.0 59.4 %all-gather.9.cloned.1.call-start = ((), (), s32[]{:S(2)}) async-start(), calls=%async_computation.2 | async-start | bytes 1769472 | tf_op jit(solution)/shard_map/all_gather | solution.py:358
  10.8 84.9 %all-gather.7.cloned.1.call-start = ((), (), s32[]{:S(2)}) async-start(), calls=%async_computation.1 | async-start | bytes 1769472 | tf_op jit(solution)/shard_map/all_gather | solution.py:362
  19.8 4.4 %copy-start.10 = (f32[1,2,192]{2,1,0:T(2,128)S(1)}, f32[1,2,192]{2,1,0:T(2,128)}, u32[]{:S(2)}) copy-start(f32[1,2,192]{2,1,0:T(2,128)} %param.9) | copy-start | bytes 4612
  19.8 5.2 %copy-start.11 = (f32[1,2,192]{2,1,0:T(2,128)S(1)}, f32[1,2,192]{2,1,0:T(2,128)}, u32[]{:S(2)}) copy-start(f32[1,2,192]{2,1,0:T(2,128)} %param.10) | copy-start | bytes 4612
  19.8 6.0 %copy-start.12 = (f32[1,2,192]{2,1,0:T(2,128)S(1)}, f32[1,2,192]{2,1,0:T(2,128)}, u32[]{:S(2)}) copy-start(f32[1,2,192]{2,1,0:T(2,128)} %param.11) | copy-start | bytes 4612
  30.6 6.6 %copy-start.13 = (s32[4]{0:T(128)S(1)}, s32[4]{0:T(128)}, u32[]{:S(2)}) copy-start(s32[4]{0:T(128)} %pad.15.clone) | copy-start | bytes 52
  76.2 14.3 %collective-permute-start = (bf16[8,192,128]{2,1,0:T(8,128)(2,1)}, bf16[8,192,128]{2,1,0:T(8,128)(2,1)S(1)}, u32[]{:S(2)}, u32[]{:S(2)}) collective-permute-start(bf16[8,192,128]{2,1,0:T(8,128)(2,1)} %get-tuple-element.32), channel_id=1, source_target_pairs={{0,8},{8,16},{16,24},{1,9},{9,17},{17,25},{2,10},{10,18},{18,26},{... | collective-permute-start | bytes 1179656 | tf_op jit(solution)/shard_map/ppermute | solution.py:404
  90.5 5.2 %copy-start.1 = (bf16[8,192,128]{2,1,0:T(8,128)(2,1)}, bf16[8,192,128]{2,1,0:T(8,128)(2,1)S(1)}, u32[]{:S(2)}) copy-start(bf16[8,192,128]{2,1,0:T(8,128)(2,1)S(1)} %collective-permute-done.src_b) | copy-start | bytes 1179652
  90.5 5.2 %collective-permute-start.1 = (bf16[8,192,128]{2,1,0:T(8,128)(2,1)S(1)}, bf16[8,192,128]{2,1,0:T(8,128)(2,1)S(1)}, u32[]{:S(2)}, u32[]{:S(2)}) collective-permute-start(bf16[8,192,128]{2,1,0:T(8,128)(2,1)S(1)} %collective-permute-done.src_b), channel_id=1, source_target_pairs={{0,1},{1,0},{2,3},{3,2},{4,5},{5,4},{6,7},{7,6},{8,9},{9,8},{10,11... | collective-permute-start | bytes 1179656 | tf_op jit(solution)/shard_map/ppermute | solution.py:406
  95.7 0.8 copy-start.4
  113.5 14.3 %collective-permute-start.2 = (bf16[8,192,128]{2,1,0:T(8,128)(2,1)}, bf16[8,192,128]{2,1,0:T(8,128)(2,1)S(1)}, u32[]{:S(2)}, u32[]{:S(2)}) collective-permute-start(bf16[8,192,128]{2,1,0:T(8,128)(2,1)} %get-tuple-element.37), channel_id=1, source_target_pairs={{0,8},{8,16},{16,24},{1,9},{9,17},{17,25},{2,10},{10,18},{18,26},{... | collective-permute-start | bytes 1179656 | tf_op jit(solution)/shard_map/ppermute | solution.py:404
  127.7 1.7 copy-start.2
  127.7 1.7 collective-permute-start.3
  129.4 0.7 copy-start.5
  147.2 14.2 %collective-permute-start.4 = (bf16[8,192,128]{2,1,0:T(8,128)(2,1)}, bf16[8,192,128]{2,1,0:T(8,128)(2,1)S(1)}, u32[]{:S(2)}, u32[]{:S(2)}) collective-permute-start(bf16[8,192,128]{2,1,0:T(8,128)(2,1)} %get-tuple-element.42), channel_id=1, source_target_pairs={{0,8},{8,16},{16,24},{1,9},{9,17},{17,25},{2,10},{10,18},{18,26},{... | collective-permute-start | bytes 1179656 | tf_op jit(solution)/shard_map/ppermute | solution.py:404
  161.4 1.7 copy-start.3
  161.4 1.7 collective-permute-start.5
  163.1 0.7 copy-start.6
  180.9 14.2 %collective-permute-start.6 = (bf16[8,192,128]{2,1,0:T(8,128)(2,1)}, bf16[8,192,128]{2,1,0:T(8,128)(2,1)S(1)}, u32[]{:S(2)}, u32[]{:S(2)}) collective-permute-start(bf16[8,192,128]{2,1,0:T(8,128)(2,1)} %get-tuple-element.46), channel_id=1, source_target_pairs={{0,8},{8,16},{16,24},{1,9},{9,17},{17,25},{2,10},{10,18},{18,26},{... | collective-permute-start | bytes 1179656 | tf_op jit(solution)/shard_map/ppermute | solution.py:404
  183.0 12.0 %copy-start = (bf16[1,2,16,192,128]{4,3,2,1,0:T(8,128)(2,1)S(1)}, bf16[1,2,16,192,128]{4,3,2,1,0:T(8,128)(2,1)}, u32[]{:S(2)}) copy-start(bf16[1,2,16,192,128]{4,3,2,1,0:T(8,128)(2,1)} %all-gather.9.cloned.1.call-done) | copy-start | bytes 4718596
  189.9 6.1 %copy-start.9 = (bf16[8,192,128]{2,1,0:T(8,128)(2,1)S(1)}, bf16[8,192,128]{2,1,0:T(8,128)(2,1)}, u32[]{:S(2)}) copy-start(bf16[8,192,128]{2,1,0:T(8,128)(2,1)} %shard_map.82) | copy-start | bytes 1179652
  195.0 2.3 copy-start.7
  195.0 2.2 collective-permute-start.7
  197.3 0.8 copy-start.8
  198.1 10.3 %slice-start = ((bf16[3,16,192,128]{3,2,1,0:T(8,128)(2,1)}), bf16[1,16,192,128]{3,2,1,0:T(8,128)(2,1)S(1)}, s32[]{:S(2)}) async-start(bf16[3,16,192,128]{3,2,1,0:T(8,128)(2,1)} %all-gather.5.cloned.1.call-done.caches.frames), calls=%async_computation.3 | async-start | bytes 1572864 | tf_op jit(solution)/shard_map/slice | solution.py:410
Sparse Core Ops, SparseCore 0:
  10.2 32.8 all-gather.4
  45.2 24.1 all-gather.8
  71.0 24.5 all-gather.6

commit v2 on v0

--- a/solution.py
+++ b/solution.py
@@ -188,19 +188,19 @@
         for i, (a, b) in enumerate(pairs):
             pltpu.make_async_copy(a, b, sems.at[base + i]).wait()
 
+    @pl.when(mode == 0)
+    def _():
+        begin([(whole.at[pl.ds(0, half)], top), (whole.at[pl.ds(half, half)], bottom)], 0)
+
+    @pl.when(mode == 1)
+    def _():
+        begin([(src_b, top), (src_c, bottom)], 0)
+
+    @pl.when(mode == 2)
+    def _():
+        begin([(src_c, top), (src_b, bottom)], 0)
+
     pltpu.make_async_copy(taps, tapbuf, sems.at[4]).start()
-
-    @pl.when(mode == 0)
-    def _():
-        begin([(whole.at[pl.ds(0, half)], top), (whole.at[pl.ds(half, half)], bottom)], 0)
-
-    @pl.when(mode == 1)
-    def _():
-        begin([(src_b, top), (src_c, bottom)], 0)
-
-    @pl.when(mode == 2)
-    def _():
-        begin([(src_c, top), (src_b, bottom)], 0)
 
     @pl.when(first == 1)
     def _():

time: 235 us -> 232 us (0.987)
  Pallas kernels: 116 us -> 113 us
    pallas_call x14, Pallas kernels: 116 us -> 113 us  [fused_conv(): pl.pallas_call(body, out_shape=shapes, in_specs=specs, out_specs=vmem if...]
  transfers between devices with their start and end apart: 11 -> 11, of which waited for: 9 -> 9; matrix products, arithmetic and copies ran while one was open for 14% -> 15% of each run, Pallas kernels for 20% -> 20%
where the time goes in v2:
time: 232 us; the launch traced here: 228 us
  Pallas kernels  113 us (49%)
  waiting for transfers between devices  43.6 us (19%)
  local copies, waits for them, and re-layouts  36.3 us (16%)
  between operations  14.3 us (6%)
  starting transfers between devices  12.4 us (5%)
  other arithmetic  8.39 us (4%)
    pallas_call x14, Pallas kernels, fused_conv(): pl.pallas_call(body, out_shape=shapes, in_specs=specs, out_specs=vmem if...  113 us
    ppermute x4, waiting for transfers between devices, shards_whole(): got = lax.ppermute(lead, 'phase', forward)  16.8 us
    all_gather x1, waiting for transfers between devices, shards_whole(): second_cache = lax.all_gather(cache_t[1], 'rows', axis=1, tiled=True)  14.5 us
    ppermute x4, starting transfers between devices, shards_whole(): got = lax.ppermute(lead, 'phase', forward)  12.2 us
    transpose x3, local copies, waits for them, and re-layouts, arrange_taps(): jnp.transpose(weight, (2, 3, 0, 1, 4)).reshape(3 * outputs, 9 * channels)  11 us
    reshape x2, local copies, waits for them, and re-layouts, arrange_taps(): jnp.transpose(weight, (2, 3, 0, 1, 4)).reshape(3 * outputs, 9 * channels)  8.65 us
    unnamed x32, local copies, waits for them, and re-layouts  7.07 us
    all_gather x1, waiting for transfers between devices, shards_whole(): lax.all_gather(jnp.stack(later), 'rows', axis=1, tiled=True)  5.07 us
  transfers between devices with their start and end apart: 11, of which 9 were waited for; matrix products, arithmetic and copies ran while one was open for 15% of the time, Pallas kernels for 20%

profile of v2, /device:TPU:4, one launch (start us, length us, event | category | flops | bytes accessed | tf_op | source)
XLA Modules:
  0.0 228.0 jit_solution(8933807606867683963)
XLA Ops:
  7.2 1.0 copy.64
  8.3 1.0 copy.65
  12.8 4.7 %slice_bitcast_fusion = (bf16[3,192,3,3,192]{4,1,0,3,2:T(8,128)(2,1)S(1)}, bf16[3,192,3,3,192]{4,1,0,3,2:T(8,128)(2,1)}) fusion(bf16[1,2,3,3,3,192,192]{6,5,4,3,2,1,0:T(8,128)(2,1)} %param.8), kind=kLoop, calls=%fused_computation | loop fusion | bytes 7962624 | tf_op jit(solution)/shard_map/transpose | solution.py:77
  17.5 2.3 copy.17
  19.8 4.4 %reshape.59.taps = bf16[576,1728]{1,0:T(8,128)(2,1)} reshape(bf16[3,192,3,3,192]{4,3,2,1,0:T(4,128)(2,1)S(1)} %copy.17) | data formatting | bytes 3981312 | tf_op jit(solution)/shard_map/reshape | solution.py:77
  24.2 0.8 copy.18.bias
  25.0 0.8 copy.19.gain
  26.5 4.1 %copy.16 = bf16[3,192,3,3,192]{4,3,2,1,0:T(4,128)(2,1)S(1)} copy(bf16[3,192,3,3,192]{4,1,0,3,2:T(8,128)(2,1)} %get-tuple-element.63) | data formatting | bytes 3981312 | tf_op jit(solution)/shard_map/transpose | solution.py:77
  30.6 4.2 %reshape.58.taps = bf16[576,1728]{1,0:T(8,128)(2,1)} reshape(bf16[3,192,3,3,192]{4,3,2,1,0:T(4,128)(2,1)S(1)} %copy.16) | data formatting | bytes 3981312 | tf_op jit(solution)/shard_map/reshape | solution.py:77
  34.9 0.8 copy.21.bias
  37.2 1.3 add_add_fusion.flags
  38.5 0.8 compare_convert_fusion.member
  39.3 3.8 %all-gather.5.cloned.1.call-done.caches.frames = bf16[3,16,192,128]{3,2,1,0:T(8,128)(2,1)} async-done(((bf16[3,2,192,128]{3,2,1,0:T(8,128)(2,1)}), bf16[3,16,192,128]{3,2,1,0:T(8,128)(2,1)}) %all-gather.5.cloned.1.call-update) | async-done | bytes 2359312 | tf_op jit(solution)/shard_map/all_gather | solution.py:342
  43.0 1.2 broadcast_in_dim.8.a_p.a_pp
  44.2 0.8 broadcast_in_dim.9.src_b.src_c
  45.0 10.0 %shard_map.77 = (bf16[16,192,128]{2,1,0:T(8,128)(2,1)}, bf16[18,192,128]{2,1,0:T(8,128)(2,1)}) custom-call(s32[5,4]{1,0:T(8,128)} %add_add_fusion.flags, bf16[3,16,192,128]{3,2,1,0:T(8,128)(2,1)} %all-gather.5.cloned.1.call-done.caches.frames, bf16[18,192,128]{2,1,0:T(8,128)(2,1)} %broadcast_in_dim.8.a_p.a_pp, ...), custom_call_target="tpu_custom_call" | custom-call | tf_op jit(solution)/shard_map/pallas_call | solution.py:286
  55.0 14.5 %all-gather.9.cloned.1.call-done = bf16[1,2,16,192,128]{4,3,2,1,0:T(8,128)(2,1)} async-done(((bf16[1,2,2,192,128]{4,3,2,1,0:T(8,128)(2,1)}), bf16[1,2,16,192,128]{4,3,2,1,0:T(8,128)(2,1)}) %all-gather.9.cloned.1.call-update) | async-done | bytes 1572880 | tf_op jit(solution)/shard_map/all_gather | solution.py:343
  69.4 6.9 %shard_map.78 = (bf16[8,192,128]{2,1,0:T(8,128)(2,1)}, bf16[18,192,128]{2,1,0:T(8,128)(2,1)}) custom-call(s32[5,4]{1,0:T(8,128)} %add_add_fusion.flags, bf16[2,16,192,128]{3,2,1,0:T(8,128)(2,1)} %bitcast.111, bf16[18,192,128]{2,1,0:T(8,128)(2,1)} %broadcast_in_dim.8.a_p.a_pp, bf16[18,192,128]{2,1,0:T(8,128)(2,1)} %broadcast_in_dim.8.a_p.a_pp, ...), custom_call_target="tpu_custom_call" | custom-call | tf_op jit(solution)/shard_map/pallas_call | solution.py:286
  76.3 3.6 %collective-permute-start = (bf16[8,192,128]{2,1,0:T(8,128)(2,1)}, bf16[8,192,128]{2,1,0:T(8,128)(2,1)S(1)}, u32[]{:S(2)}, u32[]{:S(2)}) collective-permute-start(bf16[8,192,128]{2,1,0:T(8,128)(2,1)} %get-tuple-element.32), channel_id=1, source_target_pairs={{0,8},{8,16},{16,24},{1,9},{9,17},{17,25},{2,10},{10,18},{18,26},{... | collective-permute-start | bytes 1179656 | tf_op jit(solution)/shard_map/ppermute | solution.py:389
  79.9 6.9 %shard_map.79 = bf16[8,192,128]{2,1,0:T(8,128)(2,1)} custom-call(s32[5,4]{1,0:T(8,128)} %add_add_fusion.flags, bf16[2,16,192,128]{3,2,1,0:T(8,128)(2,1)} %bitcast.112, bf16[18,192,128]{2,1,0:T(8,128)(2,1)} %broadcast_in_dim.8.a_p.a_pp, bf16[18,192,128]{2,1,0:T(8,128)(2,1)} %broadcast_in_dim.8.a_p.a_pp, ...), custom_call_target="tpu_custom_call" | custom-call | tf_op jit(solution)/shard_map/pallas_call | solution.py:286
  86.9 3.7 %collective-permute-done.src_b = bf16[8,192,128]{2,1,0:T(8,128)(2,1)S(1)} collective-permute-done((bf16[8,192,128]{2,1,0:T(8,128)(2,1)}, bf16[8,192,128]{2,1,0:T(8,128)(2,1)S(1)}, u32[]{:S(2)}, u32[]{:S(2)}) %collective-permute-start) | collective-permute-done | bytes 393248 | tf_op jit(solution)/shard_map/ppermute | solution.py:389
  90.6 5.1 %all-gather.7.cloned.1.call-done.frames = bf16[2,16,192,128]{3,2,1,0:T(8,128)(2,1)} async-done(((bf16[2,2,192,128]{3,2,1,0:T(8,128)(2,1)}), bf16[2,16,192,128]{3,2,1,0:T(8,128)(2,1)}) %all-gather.7.cloned.1.call-update) | async-done | bytes 1572880 | tf_op jit(solution)/shard_map/all_gather | solution.py:347
  96.4 9.6 %shard_map.80 = (bf16[16,192,128]{2,1,0:T(8,128)(2,1)}, bf16[18,192,128]{2,1,0:T(8,128)(2,1)}) custom-call(s32[5,4]{1,0:T(8,128)} %add_add_fusion.flags, bf16[3,16,192,128]{3,2,1,0:T(8,128)(2,1)} %all-gather.5.cloned.1.call-done.caches.frames, bf16[18,192,128]{2,1,0:T(8,128)(2,1)} %get-tuple-element.34.a_p.a_pp, ...), custom_call_target="tpu_custom_call" | custom-call | tf_op jit(solution)/shard_map/pallas_call | solution.py:286
  106.1 6.9 %shard_map.81 = (bf16[8,192,128]{2,1,0:T(8,128)(2,1)}, bf16[18,192,128]{2,1,0:T(8,128)(2,1)}) custom-call(s32[5,4]{1,0:T(8,128)} %add_add_fusion.flags, bf16[2,16,192,128]{3,2,1,0:T(8,128)(2,1)} %bitcast.113, bf16[18,192,128]{2,1,0:T(8,128)(2,1)} %get-tuple-element.31.rest_0_.a_p.a_pp, bf16[18,192,128]{2,1,0:T(8,128)(2,1)} %broadcast_in_dim.8.a_p.a_pp, ...), custom_call_target="tpu_custom_call" | custom-call | tf_op jit(solution)/shard_map/pallas_call | solution.py:286
  113.0 3.8 %collective-permute-start.2 = (bf16[8,192,128]{2,1,0:T(8,128)(2,1)}, bf16[8,192,128]{2,1,0:T(8,128)(2,1)S(1)}, u32[]{:S(2)}, u32[]{:S(2)}) collective-permute-start(bf16[8,192,128]{2,1,0:T(8,128)(2,1)} %get-tuple-element.37), channel_id=1, source_target_pairs={{0,8},{8,16},{16,24},{1,9},{9,17},{17,25},{2,10},{10,18},{18,26},{... | collective-permute-start | bytes 1179656 | tf_op jit(solution)/shard_map/ppermute | solution.py:389
  116.8 6.9 %shard_map.82 = bf16[8,192,128]{2,1,0:T(8,128)(2,1)} custom-call(s32[5,4]{1,0:T(8,128)} %add_add_fusion.flags, bf16[2,16,192,128]{3,2,1,0:T(8,128)(2,1)} %bitcast.114, bf16[18,192,128]{2,1,0:T(8,128)(2,1)} %get-tuple-element.31.rest_0_.a_p.a_pp, bf16[18,192,128]{2,1,0:T(8,128)(2,1)} %broadcast_in_dim.8.a_p.a_pp, ...), custom_call_target="tpu_custom_call" | custom-call | tf_op jit(solution)/shard_map/pallas_call | solution.py:286
  123.7 3.5 %collective-permute-done.2.src_b = bf16[8,192,128]{2,1,0:T(8,128)(2,1)S(1)} collective-permute-done((bf16[8,192,128]{2,1,0:T(8,128)(2,1)}, bf16[8,192,128]{2,1,0:T(8,128)(2,1)S(1)}, u32[]{:S(2)}, u32[]{:S(2)}) %collective-permute-start.2) | collective-permute-done | bytes 393248 | tf_op jit(solution)/shard_map/ppermute | solution.py:389
  127.2 1.7 collective-permute-done.3.src_c
  129.7 9.6 %shard_map.83 = (bf16[16,192,128]{2,1,0:T(8,128)(2,1)}, bf16[18,192,128]{2,1,0:T(8,128)(2,1)}) custom-call(s32[5,4]{1,0:T(8,128)} %add_add_fusion.flags, bf16[3,16,192,128]{3,2,1,0:T(8,128)(2,1)} %all-gather.5.cloned.1.call-done.caches.frames, bf16[18,192,128]{2,1,0:T(8,128)(2,1)} %get-tuple-element.39.a_p.a_pp, ...), custom_call_target="tpu_custom_call" | custom-call | tf_op jit(solution)/shard_map/pallas_call | solution.py:286
  139.3 6.9 %shard_map.84 = (bf16[8,192,128]{2,1,0:T(8,128)(2,1)}, bf16[18,192,128]{2,1,0:T(8,128)(2,1)}) custom-call(s32[5,4]{1,0:T(8,128)} %add_add_fusion.flags, bf16[2,16,192,128]{3,2,1,0:T(8,128)(2,1)} %bitcast.115, bf16[18,192,128]{2,1,0:T(8,128)(2,1)} %get-tuple-element.36.rest_0_.a_p.a_pp, bf16[18,192,128]{2,1,0:T(8,128)(2,1)} %get-tuple-element.31.rest_0_.a_p.a_pp, ...), custom_call_target="tpu_custom_call" | custom-call | tf_op jit(solution)/shard_map/pallas_call | solution.py:286
  146.2 2.7 %collective-permute-start.4 = (bf16[8,192,128]{2,1,0:T(8,128)(2,1)}, bf16[8,192,128]{2,1,0:T(8,128)(2,1)S(1)}, u32[]{:S(2)}, u32[]{:S(2)}) collective-permute-start(bf16[8,192,128]{2,1,0:T(8,128)(2,1)} %get-tuple-element.42), channel_id=1, source_target_pairs={{0,8},{8,16},{16,24},{1,9},{9,17},{17,25},{2,10},{10,18},{18,26},{... | collective-permute-start | bytes 1179656 | tf_op jit(solution)/shard_map/ppermute | solution.py:389
  148.9 6.9 %shard_map.85 = bf16[8,192,128]{2,1,0:T(8,128)(2,1)} custom-call(s32[5,4]{1,0:T(8,128)} %add_add_fusion.flags, bf16[2,16,192,128]{3,2,1,0:T(8,128)(2,1)} %bitcast.116, bf16[18,192,128]{2,1,0:T(8,128)(2,1)} %get-tuple-element.36.rest_0_.a_p.a_pp, bf16[18,192,128]{2,1,0:T(8,128)(2,1)} %get-tuple-element.31.rest_0_.a_p.a_pp, ...), custom_call_target="tpu_custom_call" | custom-call | tf_op jit(solution)/shard_map/pallas_call | solution.py:286
  155.8 4.6 %collective-permute-done.4.src_b = bf16[8,192,128]{2,1,0:T(8,128)(2,1)S(1)} collective-permute-done((bf16[8,192,128]{2,1,0:T(8,128)(2,1)}, bf16[8,192,128]{2,1,0:T(8,128)(2,1)S(1)}, u32[]{:S(2)}, u32[]{:S(2)}) %collective-permute-start.4) | collective-permute-done | bytes 393248 | tf_op jit(solution)/shard_map/ppermute | solution.py:389
  160.4 1.7 collective-permute-done.5.src_c
  162.9 9.7 %shard_map.86 = (bf16[16,192,128]{2,1,0:T(8,128)(2,1)}, bf16[18,192,128]{2,1,0:T(8,128)(2,1)}) custom-call(s32[5,4]{1,0:T(8,128)} %add_add_fusion.flags, bf16[3,16,192,128]{3,2,1,0:T(8,128)(2,1)} %all-gather.5.cloned.1.call-done.caches.frames, bf16[18,192,128]{2,1,0:T(8,128)(2,1)} %get-tuple-element.44.a_p.a_pp, ...), custom_call_target="tpu_custom_call" | custom-call | tf_op jit(solution)/shard_map/pallas_call | solution.py:286
  172.5 6.9 %shard_map.87 = (bf16[8,192,128]{2,1,0:T(8,128)(2,1)}, bf16[18,192,128]{2,1,0:T(8,128)(2,1)}) custom-call(s32[5,4]{1,0:T(8,128)} %add_add_fusion.flags, bf16[2,16,192,128]{3,2,1,0:T(8,128)(2,1)} %bitcast.117, bf16[18,192,128]{2,1,0:T(8,128)(2,1)} %get-tuple-element.41.rest_0_.a_p.a_pp, bf16[18,192,128]{2,1,0:T(8,128)(2,1)} %get-tuple-element.36.rest_0_.a_p.a_pp, ...), custom_call_target="tpu_custom_call" | custom-call | tf_op jit(solution)/shard_map/pallas_call | solution.py:286
  179.4 2.1 collective-permute-start.6
  181.6 7.0 %shard_map.88 = bf16[8,192,128]{2,1,0:T(8,128)(2,1)} custom-call(s32[5,4]{1,0:T(8,128)} %add_add_fusion.flags, bf16[2,16,192,128]{3,2,1,0:T(8,128)(2,1)} %bitcast.118, bf16[18,192,128]{2,1,0:T(8,128)(2,1)} %get-tuple-element.41.rest_0_.a_p.a_pp, bf16[18,192,128]{2,1,0:T(8,128)(2,1)} %get-tuple-element.36.rest_0_.a_p.a_pp, ...), custom_call_target="tpu_custom_call" | custom-call | tf_op jit(solution)/shard_map/pallas_call | solution.py:286
  188.6 5.0 %collective-permute-done.6.src_b = bf16[8,192,128]{2,1,0:T(8,128)(2,1)S(1)} collective-permute-done((bf16[8,192,128]{2,1,0:T(8,128)(2,1)}, bf16[8,192,128]{2,1,0:T(8,128)(2,1)S(1)}, u32[]{:S(2)}, u32[]{:S(2)}) %collective-permute-start.6) | collective-permute-done | bytes 393248 | tf_op jit(solution)/shard_map/ppermute | solution.py:389
  193.6 1.0 slice.52
  194.6 1.2 select_bitcast_fusion.3
  196.6 9.7 %shard_map.89 = (bf16[16,192,128]{2,1,0:T(8,128)(2,1)}, bf16[18,192,128]{2,1,0:T(8,128)(2,1)}) custom-call(s32[5,4]{1,0:T(8,128)} %add_add_fusion.flags, bf16[3,16,192,128]{3,2,1,0:T(8,128)(2,1)} %all-gather.5.cloned.1.call-done.caches.frames, bf16[18,192,128]{2,1,0:T(8,128)(2,1)} %get-tuple-element.53.a_p, ...), custom_call_target="tpu_custom_call" | custom-call | tf_op jit(solution)/shard_map/pallas_call | solution.py:286
  206.3 1.1 fusion.7
  207.5 9.2 %shard_map.90 = (bf16[16,192,128]{2,1,0:T(8,128)(2,1)}, bf16[18,192,128]{2,1,0:T(8,128)(2,1)}) custom-call(s32[5,4]{1,0:T(8,128)} %add_add_fusion.flags, bf16[2,16,192,128]{3,2,1,0:T(8,128)(2,1)} %bitcast.119, bf16[18,192,128]{2,1,0:T(8,128)(2,1)} %get-tuple-element.47.rest_0_.a_p, bf16[18,192,128]{2,1,0:T(8,128)(2,1)} %get-tuple-element.41.rest_0_.a_p.a_pp, ...), custom_call_target="tpu_custom_call" | custom-call | tf_op jit(solution)/shard_map/pallas_call | solution.py:286
  216.7 1.2 fusion.1
  218.0 1.2 copy.61
  219.1 1.2 select_bitcast_fusion.2
  220.4 0.9 copy.60
  (61 shorter events, 9.1 us)
Async XLA Ops:
  7.2 35.9 %all-gather.5.cloned.1.call-start = ((), (), s32[]{:S(2)}) async-start(), calls=%async_computation | async-start | bytes 2654208 | tf_op jit(solution)/shard_map/all_gather | solution.py:342
  10.0 59.4 %all-gather.9.cloned.1.call-start = ((), (), s32[]{:S(2)}) async-start(), calls=%async_computation.2 | async-start | bytes 1769472 | tf_op jit(solution)/shard_map/all_gather | solution.py:343
  10.8 84.9 %all-gather.7.cloned.1.call-start = ((), (), s32[]{:S(2)}) async-start(), calls=%async_computation.1 | async-start | bytes 1769472 | tf_op jit(solution)/shard_map/all_gather | solution.py:347
  19.8 4.4 %copy-start.10 = (f32[1,2,192]{2,1,0:T(2,128)S(1)}, f32[1,2,192]{2,1,0:T(2,128)}, u32[]{:S(2)}) copy-start(f32[1,2,192]{2,1,0:T(2,128)} %param.9) | copy-start | bytes 4612
  19.8 5.2 %copy-start.11 = (f32[1,2,192]{2,1,0:T(2,128)S(1)}, f32[1,2,192]{2,1,0:T(2,128)}, u32[]{:S(2)}) copy-start(f32[1,2,192]{2,1,0:T(2,128)} %param.10) | copy-start | bytes 4612
  19.8 6.0 %copy-start.12 = (f32[1,2,192]{2,1,0:T(2,128)S(1)}, f32[1,2,192]{2,1,0:T(2,128)}, u32[]{:S(2)}) copy-start(f32[1,2,192]{2,1,0:T(2,128)} %param.11) | copy-start | bytes 4612
  30.6 6.6 %copy-start.13 = (s32[4]{0:T(128)S(1)}, s32[4]{0:T(128)}, u32[]{:S(2)}) copy-start(s32[4]{0:T(128)} %pad.15.clone) | copy-start | bytes 52
  76.3 14.3 %collective-permute-start = (bf16[8,192,128]{2,1,0:T(8,128)(2,1)}, bf16[8,192,128]{2,1,0:T(8,128)(2,1)S(1)}, u32[]{:S(2)}, u32[]{:S(2)}) collective-permute-start(bf16[8,192,128]{2,1,0:T(8,128)(2,1)} %get-tuple-element.32), channel_id=1, source_target_pairs={{0,8},{8,16},{16,24},{1,9},{9,17},{17,25},{2,10},{10,18},{18,26},{... | collective-permute-start | bytes 1179656 | tf_op jit(solution)/shard_map/ppermute | solution.py:389
  90.6 5.1 %copy-start.1 = (bf16[8,192,128]{2,1,0:T(8,128)(2,1)}, bf16[8,192,128]{2,1,0:T(8,128)(2,1)S(1)}, u32[]{:S(2)}) copy-start(bf16[8,192,128]{2,1,0:T(8,128)(2,1)S(1)} %collective-permute-done.src_b) | copy-start | bytes 1179652
  90.6 5.1 %collective-permute-start.1 = (bf16[8,192,128]{2,1,0:T(8,128)(2,1)S(1)}, bf16[8,192,128]{2,1,0:T(8,128)(2,1)S(1)}, u32[]{:S(2)}, u32[]{:S(2)}) collective-permute-start(bf16[8,192,128]{2,1,0:T(8,128)(2,1)S(1)} %collective-permute-done.src_b), channel_id=1, source_target_pairs={{0,1},{1,0},{2,3},{3,2},{4,5},{5,4},{6,7},{7,6},{8,9},{9,8},{10,11... | collective-permute-start | bytes 1179656 | tf_op jit(solution)/shard_map/ppermute | solution.py:391
  95.7 0.8 copy-start.4
  113.0 14.3 %collective-permute-start.2 = (bf16[8,192,128]{2,1,0:T(8,128)(2,1)}, bf16[8,192,128]{2,1,0:T(8,128)(2,1)S(1)}, u32[]{:S(2)}, u32[]{:S(2)}) collective-permute-start(bf16[8,192,128]{2,1,0:T(8,128)(2,1)} %get-tuple-element.37), channel_id=1, source_target_pairs={{0,8},{8,16},{16,24},{1,9},{9,17},{17,25},{2,10},{10,18},{18,26},{... | collective-permute-start | bytes 1179656 | tf_op jit(solution)/shard_map/ppermute | solution.py:389
  127.2 1.7 copy-start.2
  127.2 1.7 collective-permute-start.3
  128.9 0.7 copy-start.5
  146.2 14.2 %collective-permute-start.4 = (bf16[8,192,128]{2,1,0:T(8,128)(2,1)}, bf16[8,192,128]{2,1,0:T(8,128)(2,1)S(1)}, u32[]{:S(2)}, u32[]{:S(2)}) collective-permute-start(bf16[8,192,128]{2,1,0:T(8,128)(2,1)} %get-tuple-element.42), channel_id=1, source_target_pairs={{0,8},{8,16},{16,24},{1,9},{9,17},{17,25},{2,10},{10,18},{18,26},{... | collective-permute-start | bytes 1179656 | tf_op jit(solution)/shard_map/ppermute | solution.py:389
  160.4 1.7 copy-start.3
  160.4 1.7 collective-permute-start.5
  162.1 0.7 copy-start.6
  179.4 14.2 %collective-permute-start.6 = (bf16[8,192,128]{2,1,0:T(8,128)(2,1)}, bf16[8,192,128]{2,1,0:T(8,128)(2,1)S(1)}, u32[]{:S(2)}, u32[]{:S(2)}) collective-permute-start(bf16[8,192,128]{2,1,0:T(8,128)(2,1)} %get-tuple-element.46), channel_id=1, source_target_pairs={{0,8},{8,16},{16,24},{1,9},{9,17},{17,25},{2,10},{10,18},{18,26},{... | collective-permute-start | bytes 1179656 | tf_op jit(solution)/shard_map/ppermute | solution.py:389
  181.6 12.0 %copy-start = (bf16[1,2,16,192,128]{4,3,2,1,0:T(8,128)(2,1)S(1)}, bf16[1,2,16,192,128]{4,3,2,1,0:T(8,128)(2,1)}, u32[]{:S(2)}) copy-start(bf16[1,2,16,192,128]{4,3,2,1,0:T(8,128)(2,1)} %all-gather.9.cloned.1.call-done) | copy-start | bytes 4718596
  188.6 6.0 %copy-start.9 = (bf16[8,192,128]{2,1,0:T(8,128)(2,1)S(1)}, bf16[8,192,128]{2,1,0:T(8,128)(2,1)}, u32[]{:S(2)}) copy-start(bf16[8,192,128]{2,1,0:T(8,128)(2,1)} %shard_map.82) | copy-start | bytes 1179652
  193.6 2.3 copy-start.7
  193.6 2.2 collective-permute-start.7
  195.8 0.8 copy-start.8
  196.6 9.7 %slice-start = ((bf16[3,16,192,128]{3,2,1,0:T(8,128)(2,1)}), bf16[1,16,192,128]{3,2,1,0:T(8,128)(2,1)S(1)}, s32[]{:S(2)}) async-start(bf16[3,16,192,128]{3,2,1,0:T(8,128)(2,1)} %all-gather.5.cloned.1.call-done.caches.frames), calls=%async_computation.3 | async-start | bytes 1572864 | tf_op jit(solution)/shard_map/slice | solution.py:395
Sparse Core Ops, SparseCore 0:
  10.2 32.8 all-gather.4
  45.2 24.1 all-gather.8
  71.0 24.5 all-gather.6
